TPU v7x, 256 devices: a whole 4x4x8 slice. The times are simulated.
256 devices in a mesh: gx: 8 (over y, core), gy: 32 (over x, z).
Axes of the slice: x: 4, y: 4, z: 8, core: 2. Of those that a mesh axis runs over, the one named last changes fastest.
Arguments:
- inputs: bfloat16 [3072, 7168], P('gy', 'gx'), may hold values from -6 to 6
- query_weight: bfloat16 [7168, 7168], P('gy', 'gx'), may hold values from -0.0625 to 0.0625
- key_weight: bfloat16 [7168, 7168], P('gy', 'gx'), may hold values from -0.0625 to 0.0625
- value_weight: bfloat16 [7168, 7168], P('gy', 'gx'), may hold values from -0.0625 to 0.0625
- adapter_down: bfloat16 [128, 7168], P(None, 'gx'), may hold values from -0.0625 to 0.0625
- adapter_up: bfloat16 [7168, 128], P('gy'), may hold values from -0.5 to 0.5
- prompt_keys: bfloat16 [8, 7168, 2048], P('gx', 'gy'), may hold values from -6 to 6
- prompt_values: bfloat16 [8, 7168, 2048], P('gx', 'gy'), may hold values from -6 to 6
- cache_keys: bfloat16 [64, 7168, 512], P('gx', 'gy'), may hold values from -240 to 240
- cache_values: bfloat16 [64, 7168, 512], P('gx', 'gy'), may hold values from -6 to 6
- cache_lengths: int32 [64], P('gx'), may hold values from 1 to 512, as said below
- parents: int32 [64, 48], P('gx'), may hold values from 0 to 46, as said below
- out_weight: bfloat16 [7168, 3584], P('gy', 'gx'), may hold values from -0.125 to 0.125
Outputs:
- layer_output: bfloat16 [3072, 3584], P('gx', 'gy')
Inputs may be any that keep to these rules, and one draw needn't show every extreme that they name: `parents`: node n's parent is a node below n, node 0 is its own parent, and node 47 hangs from node 46. `cache_lengths`: some request has all 512 positions valid.
All inputs are finite; a program needn't handle non-finite values.
Results may differ from a plain program's by a relative error of at most 0.017.
Values may be sent and summed in bfloat16 or wider, within the bound.
No kernel may reach another device: no remote copies, remote signals or barrier semaphores. Data moves between devices by JAX's collectives and lax.ppermute only.
A program may use at most 128 MiB of HBM per device.

v0:
```python
import math

import jax
import jax.numpy as jnp
from jax import lax
from jax.sharding import PartitionSpec as P

HEAD = 224


def contract_rows(left, right):
    return lax.dot_general(
        left, right, (((1,), (1,)), ((), ())), preferred_element_type=jnp.float32
    )


def ancestors(parents):
    node_count = parents.shape[1]
    columns = jnp.arange(node_count, dtype=jnp.int32)
    parent_hot = (parents[:, :, None] == columns[None, None, :]).astype(jnp.float32)
    reached = jnp.minimum(jnp.eye(node_count, dtype=jnp.float32)[None] + parent_hot, 1.0)
    rounds = max(1, math.ceil(math.log2(node_count)))
    for sweep in range(rounds):
        reached = jnp.minimum(
            reached + jnp.einsum("rnm,rmk->rnk", reached, reached, precision=lax.Precision.HIGHEST),
            1.0,
        )
    return reached


def attend(queries, new_keys, new_values, prompt_k, prompt_v, cache_k, cache_v, lengths, parents):
    factor = 1.0 / math.sqrt(queries.shape[-1])
    s_prompt = (
        jnp.einsum("rnhe,hep->rnhp", queries, prompt_k, preferred_element_type=jnp.float32) * factor
    )
    s_cache = (
        jnp.einsum("rnhe,rhec->rnhc", queries, cache_k, preferred_element_type=jnp.float32) * factor
    )
    s_tree = (
        jnp.einsum("rnhe,rmhe->rnhm", queries, new_keys, preferred_element_type=jnp.float32)
        * factor
    )
    usable = jnp.arange(cache_k.shape[-1], dtype=jnp.int32)[None, :] < lengths[:, None]
    s_cache = jnp.where(usable[:, None, None, :], s_cache, -jnp.inf)
    reached = ancestors(parents)
    s_tree = jnp.where(reached[:, :, None, :] > 0.5, s_tree, -jnp.inf)
    largest = jnp.maximum(
        jnp.maximum(
            jnp.max(s_prompt, axis=-1, keepdims=True), jnp.max(s_cache, axis=-1, keepdims=True)
        ),
        jnp.max(s_tree, axis=-1, keepdims=True),
    )
    e_prompt = jnp.exp(s_prompt - largest)
    e_cache = jnp.exp(s_cache - largest)
    e_tree = jnp.exp(s_tree - largest)
    totals = (
        jnp.sum(e_prompt, axis=-1, keepdims=True)
        + jnp.sum(e_cache, axis=-1, keepdims=True)
        + jnp.sum(e_tree, axis=-1, keepdims=True)
    )
    w_prompt = (e_prompt / totals).astype(jnp.bfloat16)
    w_cache = (e_cache / totals).astype(jnp.bfloat16)
    w_tree = (e_tree / totals).astype(jnp.bfloat16)
    result = jnp.einsum("rnhp,hep->rnhe", w_prompt, prompt_v, preferred_element_type=jnp.float32)
    result = result + jnp.einsum(
        "rnhc,rhec->rnhe", w_cache, cache_v, preferred_element_type=jnp.float32
    )
    result = result + jnp.einsum(
        "rnhm,rmhe->rnhe", w_tree, new_values, preferred_element_type=jnp.float32
    )
    return result.astype(jnp.bfloat16)


def per_device(
    inputs,
    query_weight,
    key_weight,
    value_weight,
    adapter_down,
    adapter_up,
    prompt_keys,
    prompt_values,
    cache_keys,
    cache_values,
    cache_lengths,
    parents,
    out_weight,
):
    requests = cache_keys.shape[0]
    node_count = parents.shape[1]
    local_rows = requests * node_count
    head_width = query_weight.shape[0]
    all_rows = lax.all_gather(inputs, "gy", axis=0, tiled=True)
    mixture = lax.psum_scatter(
        jnp.concatenate(
            [
                contract_rows(all_rows, matrix)
                for matrix in (query_weight, key_weight, value_weight, adapter_down)
            ],
            axis=1,
        ),
        "gx",
        scatter_dimension=0,
        tiled=True,
    )
    head_count = head_width // HEAD
    query_base = mixture[:, :head_width]
    new_keys = mixture[:, head_width : 2 * head_width].astype(jnp.bfloat16)
    new_values = mixture[:, 2 * head_width : 3 * head_width].astype(jnp.bfloat16)
    adapter_mid = mixture[:, 3 * head_width :].astype(jnp.bfloat16)
    queries = (query_base + contract_rows(adapter_mid, adapter_up)).astype(jnp.bfloat16)
    shaped = (requests, node_count, head_count, HEAD)
    cached = (requests, head_count, HEAD, cache_keys.shape[2])
    attended = attend(
        queries.reshape(shaped),
        new_keys.reshape(shaped),
        new_values.reshape(shaped),
        prompt_keys,
        prompt_values,
        cache_keys.reshape(cached),
        cache_values.reshape(cached),
        cache_lengths,
        parents,
    )
    flattened = attended.reshape(local_rows, head_width)
    partial_sums = jnp.dot(
        flattened,
        lax.all_gather(out_weight, "gx", axis=1, tiled=True),
        preferred_element_type=jnp.float32,
    )
    return lax.psum_scatter(
        partial_sums.astype(jnp.bfloat16), "gy", scatter_dimension=1, tiled=True
    )


def solution(mesh):
    placed = (
        P("gy", "gx"),
        P("gy", "gx"),
        P("gy", "gx"),
        P("gy", "gx"),
        P(None, "gx"),
        P("gy", None),
        P("gx", "gy", None),
        P("gx", "gy", None),
        P("gx", "gy", None),
        P("gx", "gy", None),
        P("gx"),
        P("gx", None),
        P("gy", "gx"),
    )
    return jax.shard_map(
        per_device, mesh=mesh, in_specs=placed, out_specs=P("gx", "gy"), check_vma=False
    )
```

profile of v0, /device:TPU:8, one launch (start us, length us, event | category | flops | bytes accessed | tf_op | source)
XLA Modules:
  0.0 421.0 jit_solution(16810437612940180732)
XLA Ops:
  6.5 0.7 all-gather.3.cloned.1.call-update
  7.3 91.2 %all-gather.3.cloned.1.call-done = bf16[3072,896]{1,0:T(8,128)(2,1)} async-done(((bf16[96,896]{1,0:T(8,128)(2,1)}), bf16[3072,896]{1,0:T(8,128)(2,1)}) %all-gather.3.cloned.1.call-update) | async-done | bytes 5505040 | tf_op jit(solution)/shard_map/all_gather | solution.py:93
  98.5 4.7 %fusion.44 = f32[3072,224]{0,1:T(8,128)S(1)} fusion(bf16[3072,896]{1,0:T(8,128)(2,1)} %all-gather.3.cloned.1.call-done, bf16[224,896]{1,0:T(8,128)(2,1)} %param.14), kind=kOutput, calls=%fused_computation.68 | convolution fusion | flops 1233125376 | bytes 8658944 | tf_op jit(solution)/shard_map/dot_general | solution.py:12
  103.2 1.9 fusion.45
  105.1 1.9 fusion.46
  107.0 1.9 fusion.47
  108.9 3.9 pad_maximum_fusion
  112.9 0.8 copy-done.5
  113.8 0.8 copy.46
  114.9 0.4 fusion.14
  116.5 0.3 fusion.23
  117.0 52.5 %reduce-scatter.3.cloned.1.call-done = f32[384,800]{0,1:T(8,128)} async-done(((f32[3072,800]{0,1:T(8,128)}), f32[384,800]{0,1:T(8,128)}) %reduce-scatter.3.cloned.1.call-update) | async-done | bytes 1228816 | tf_op jit(solution)/shard_map/reduce_scatter | solution.py:94
  169.4 1.4 convert.5
  170.9 1.2 fusion.13
  172.4 0.8 copy.44
  173.5 0.5 fusion.43
  174.0 0.7 bitcast_reduce_fusion
  175.0 0.6 fusion.1
  176.0 0.7 fusion.7
  176.7 0.8 copy-done.10
  177.5 0.7 fusion.12
  178.2 21.0 %all-gather.5.cloned.1.call-done = bf16[224,3584]{0,1:T(8,128)(2,1)} async-done(((bf16[224,448]{0,1:T(8,128)(2,1)}), bf16[224,3584]{0,1:T(8,128)(2,1)}) %all-gather.5.cloned.1.call-update) | async-done | bytes 1605648 | tf_op jit(solution)/shard_map/all_gather | solution.py:128
  199.2 4.2 convolution_convert_fusion
  203.4 211.1 %reduce-scatter.5.cloned.1.call-done = bf16[384,112]{0,1:T(8,128)(2,1)} async-done(((bf16[384,3584]{0,1:T(8,128)(2,1)}), bf16[384,112]{0,1:T(8,128)(2,1)}) %reduce-scatter.5.cloned.1.call-update) | async-done | bytes 86032 | tf_op jit(solution)/shard_map/reduce_scatter | solution.py:131
  (46 shorter events, 3.0 us)
Async XLA Ops:
  6.5 166.9 %copy-start = (bf16[8,224,512]{2,1,0:T(8,128)(2,1)S(1)}, bf16[8,224,512]{2,1,0:T(8,128)(2,1)}, u32[]{:S(2)}) copy-start(bf16[8,224,512]{2,1,0:T(8,128)(2,1)} %param.21) | copy-start | bytes 5505028
  6.5 91.9 %all-gather.3.cloned.1.call-start = ((), (), s32[]{:S(2)}) async-start(), calls=%async_computation.2 | async-start | bytes 5677056 | tf_op jit(solution)/shard_map/all_gather | solution.py:93
  7.3 95.9 %copy-start.3 = (bf16[224,896]{1,0:T(8,128)(2,1)S(1)}, bf16[224,896]{1,0:T(8,128)(2,1)}, u32[]{:S(2)}) copy-start(bf16[224,896]{1,0:T(8,128)(2,1)} %param.15) | copy-start | bytes 1204228
  7.3 162.2 %reduce-scatter.3.cloned.1.call-start = ((), (), s32[]{:S(2)}) async-start(), calls=%async_computation.3 | async-start | bytes 11059200 | tf_op jit(solution)/shard_map/reduce_scatter | solution.py:94
  98.5 4.7 %copy-start.1 = (bf16[3072,896]{1,0:T(8,128)(2,1)S(1)}, bf16[3072,896]{1,0:T(8,128)(2,1)}, u32[]{:S(2)}) copy-start(bf16[3072,896]{1,0:T(8,128)(2,1)} %all-gather.3.cloned.1.call-done) | copy-start | bytes 16515076
  103.2 1.9 copy-start.4
  105.1 1.9 copy-start.6
  112.8 0.9 copy-start.5
  112.8 2.1 copy-start.12
  112.9 4.0 copy-start.9
  112.9 58.0 %copy-start.8 = (bf16[224,128]{1,0:T(8,128)(2,1)S(1)}, bf16[224,128]{1,0:T(8,128)(2,1)}, u32[]{:S(2)}) copy-start(bf16[224,128]{1,0:T(8,128)(2,1)} %param.18) | copy-start | bytes 172036
  112.9 86.3 %all-gather.5.cloned.1.call-start = ((), (), s32[]{:S(2)}) async-start(), calls=%async_computation.4 | async-start | bytes 2064384 | tf_op jit(solution)/shard_map/all_gather | solution.py:128
  114.7 299.8 %reduce-scatter.5.cloned.1.call-start = ((), (), s32[]{:S(2)}) async-start(), calls=%async_computation.5 | async-start | bytes 2838528 | tf_op jit(solution)/shard_map/reduce_scatter | solution.py:131
  170.8 3.2 copy-start.2
  174.7 0.9 copy-start.7
  174.7 1.3 copy-start.11
  176.0 1.5 copy-start.10
Sparse Core Ops, SparseCore 0:
  9.9 88.5 all-gather.2
  113.0 56.4 reduce-scatter.2
  171.3 27.8 all-gather.4
  203.5 210.9 reduce-scatter.4
where the time goes:
time: 421 us
  waiting for transfers between devices  376 us (89%)
  matrix products  20.8 us (5%)
  between operations  13.4 us (3%)
  other arithmetic  6.25 us (1%)
    reduce_scatter x1, waiting for transfers between devices, per_device(): lax.psum_scatter(partial_sums.astype(jnp.bfloat16), 'gy', scatter_dimensi...  211 us
    all_gather x1, waiting for transfers between devices, per_device(): all_rows = lax.all_gather(inputs, 'gy', axis=0, tiled=True)  91.2 us
    reduce_scatter x1, waiting for transfers between devices, per_device(): lax.psum_scatter(jnp.concatenate([contract_rows(all_rows, matrix) for mat...  52.5 us
    all_gather x1, waiting for transfers between devices, per_device(): lax.all_gather(out_weight, 'gx', axis=1, tiled=True)  21 us
    dot_general x5, matrix products, contract_rows(): lax.dot_general(left, right, (((1,), (1,)), ((), ())), preferred_element_...  11.6 us
  transfers between devices with their start and end apart: 4, of which 4 were waited for; matrix products, arithmetic and copies ran while one was open for 3% of the time, Pallas kernels for 0%

commit v1 on v0

--- a/solution.py
+++ b/solution.py
@@ -2,10 +2,13 @@
 
 import jax
 import jax.numpy as jnp
+import numpy as np
 from jax import lax
+from jax.sharding import Mesh
 from jax.sharding import PartitionSpec as P
 
 HEAD = 224
+GY = ("gyx", "gyz")
 
 
 def contract_rows(left, right):
@@ -90,7 +93,9 @@
     node_count = parents.shape[1]
     local_rows = requests * node_count
     head_width = query_weight.shape[0]
-    all_rows = lax.all_gather(inputs, "gy", axis=0, tiled=True)
+    full_columns = lax.all_gather(out_weight, "gx", axis=1, tiled=True)
+    own_block = lax.all_to_all(full_columns, "gyx", 1, 0, tiled=True)
+    all_rows = lax.all_gather(inputs, GY, axis=0, tiled=True)
     mixture = lax.psum_scatter(
         jnp.concatenate(
             [
@@ -123,32 +128,37 @@
         parents,
     )
     flattened = attended.reshape(local_rows, head_width)
-    partial_sums = jnp.dot(
-        flattened,
-        lax.all_gather(out_weight, "gx", axis=1, tiled=True),
-        preferred_element_type=jnp.float32,
-    )
-    return lax.psum_scatter(
-        partial_sums.astype(jnp.bfloat16), "gy", scatter_dimension=1, tiled=True
-    )
+    heads_along_x = lax.all_gather(flattened, "gyx", axis=1, tiled=True)
+    partial_sums = jnp.dot(heads_along_x, own_block, preferred_element_type=jnp.float32)
+    parts = lax.psum(1, "gyz")
+    pieces = partial_sums.astype(jnp.bfloat16).reshape(local_rows, parts, -1)
+    arrived = lax.all_to_all(pieces, "gyz", 1, 1, tiled=True)
+    return jnp.sum(arrived.astype(jnp.float32), axis=1).astype(jnp.bfloat16)
+
+
+def split_mesh(mesh):
+    devices = mesh.devices
+    along_x = len({d.coords[0] for d in devices[0]})
+    shape = (devices.shape[0], along_x, devices.shape[1] // along_x)
+    return Mesh(devices.reshape(shape), ("gx",) + GY)
 
 
 def solution(mesh):
     placed = (
-        P("gy", "gx"),
-        P("gy", "gx"),
-        P("gy", "gx"),
-        P("gy", "gx"),
+        P(GY, "gx"),
+        P(GY, "gx"),
+        P(GY, "gx"),
+        P(GY, "gx"),
         P(None, "gx"),
-        P("gy", None),
-        P("gx", "gy", None),
-        P("gx", "gy", None),
-        P("gx", "gy", None),
-        P("gx", "gy", None),
+        P(GY, None),
+        P("gx", GY, None),
+        P("gx", GY, None),
+        P("gx", GY, None),
+        P("gx", GY, None),
         P("gx"),
         P("gx", None),
-        P("gy", "gx"),
+        P(GY, "gx"),
     )
     return jax.shard_map(
-        per_device, mesh=mesh, in_specs=placed, out_specs=P("gx", "gy"), check_vma=False
+        per_device, mesh=split_mesh(mesh), in_specs=placed, out_specs=P("gx", GY), check_vma=False
     )

time: 421 us -> 251 us (0.60)
  waiting for transfers between devices: 376 us -> 154 us
  blocking collectives: 0 us -> 42.4 us
  starting transfers between devices: 0.31 us -> 4.58 us
    reduce_scatter x1 -> x0, waiting for transfers between devices: 211 us -> none  [per_device(): lax.psum_scatter(partial_sums.astype(jnp.bfloat16), 'gy', scatter_dimensi...]
    all_to_all x0 -> x1, blocking collectives: none -> 27.2 us  [per_device(): arrived = lax.all_to_all(pieces, 'gyz', 1, 1, tiled=True)]
    all_gather x2, waiting for transfers between devices: 112 us -> 96.9 us  [the longest x1 89.3 us: per_device(): all_rows = lax.all_gather(inputs, GY, axis=0, tiled=True)]
    all_gather x0 -> x1, blocking collectives: none -> 15.2 us  [per_device(): heads_along_x = lax.all_gather(flattened, 'gyx', axis=1, tiled=True)]
    all_to_all x0 -> x1, starting transfers between devices: none -> 4.5 us  [per_device(): own_block = lax.all_to_all(full_columns, 'gyx', 1, 0, tiled=True)]
  transfers between devices with their start and end apart: 4 -> 4, of which waited for: 4 -> 3; matrix products, arithmetic and copies ran while one was open for 3% -> 13% of each run, Pallas kernels for 0% -> 0%
where the time goes in v1:
time: 251 us
  waiting for transfers between devices  154 us (61%)
  blocking collectives  42.4 us (17%)
  matrix products  22.5 us (9%)
  between operations  13.4 us (5%)
  local copies, waits for them, and re-layouts  7.09 us (3%)
  other arithmetic  7.02 us (3%)
  starting transfers between devices  4.58 us (2%)
    all_gather x1, waiting for transfers between devices, per_device(): all_rows = lax.all_gather(inputs, GY, axis=0, tiled=True)  89.3 us
    reduce_scatter x1, waiting for transfers between devices, per_device(): lax.psum_scatter(jnp.concatenate([contract_rows(all_rows, matrix) for mat...  55.9 us
    all_to_all x1, blocking collectives, per_device(): arrived = lax.all_to_all(pieces, 'gyz', 1, 1, tiled=True)  27.2 us
    all_gather x1, blocking collectives, per_device(): heads_along_x = lax.all_gather(flattened, 'gyx', axis=1, tiled=True)  15.2 us
    dot_general x5, matrix products, contract_rows(): lax.dot_general(left, right, (((1,), (1,)), ((), ())), preferred_element_...  11.5 us
    all_gather x1, waiting for transfers between devices, per_device(): full_columns = lax.all_gather(out_weight, 'gx', axis=1, tiled=True)  7.57 us
  transfers between devices with their start and end apart: 4, of which 3 were waited for; matrix products, arithmetic and copies ran while one was open for 13% of the time, Pallas kernels for 0%

profile of v1, /device:TPU:8, one launch (start us, length us, event | category | flops | bytes accessed | tf_op | source)
XLA Modules:
  0.0 250.5 jit_solution(12985714023704259796)
XLA Ops:
  6.5 0.7 all-gather.3.cloned.1.call-update
  7.3 1.8 copy.60
  9.2 89.3 %all-gather.3.cloned.1.call-done = bf16[3072,896]{1,0:T(8,128)(2,1)} async-done(((bf16[96,896]{1,0:T(8,128)(2,1)}), bf16[3072,896]{1,0:T(8,128)(2,1)}) %all-gather.3.cloned.1.call-update) | async-done | bytes 5505040 | tf_op jit(solution)/shard_map/all_gather | solution.py:98
  98.5 4.6 %fusion.47 = f32[3072,128]{0,1:T(8,128)S(1)} fusion(bf16[3072,896]{1,0:T(8,128)(2,1)} %all-gather.3.cloned.1.call-done, bf16[128,896]{1,0:T(8,128)(2,1)} %param.17), kind=kOutput, calls=%fused_computation.71 | convolution fusion | flops 704643072 | bytes 7307264 | tf_op jit(solution)/shard_map/dot_general | solution.py:15
  103.1 1.9 fusion.44
  105.0 1.9 fusion.45
  106.9 1.9 fusion.46
  108.8 4.0 %pad_maximum_fusion = f32[3072,800]{0,1:T(8,128)} fusion(f32[3072,128]{0,1:T(8,128)S(1)} %fusion.47, f32[3072,224]{0,1:T(8,128)S(1)} %fusion.46, f32[3072,224]{0,1:T(8,128)S(1)} %fusion.45, f32[3072,224]{0,1:T(8,128)S(1)} %fusion.44), kind=kLoop, calls=%fused_computation | loop fusion | flops 7372800 | bytes 19660800 | tf_op jit(solution)/shard_map/concatenate | solution.py:100
  112.8 0.6 copy-done.9
  115.5 7.6 %all-gather.5.cloned.1.call-done = bf16[224,3584]{0,1:T(8,128)(2,1)} async-done(((bf16[224,448]{0,1:T(8,128)(2,1)}), bf16[224,3584]{0,1:T(8,128)(2,1)}) %all-gather.5.cloned.1.call-update) | async-done | bytes 1605648 | tf_op jit(solution)/shard_map/all_gather | solution.py:96
  123.1 3.6 %copy.62 = bf16[224,4,896]{2,0,1:T(8,128)(2,1)} copy(bf16[224,4,896]{0,2,1:T(8,128)(2,1)} %bitcast.120) | data formatting | bytes 3211264 | tf_op jit(solution)/shard_map/all_to_all | solution.py:97
  126.7 4.5 %all-to-all-start = ((bf16[224,4,896]{2,0,1:T(8,128)(2,1)}), bf16[224,4,896]{2,0,1:T(8,128)(2,1)}, u32[]{:S(2)}, u32[]{:S(2)}) async-start(bf16[224,4,896]{2,0,1:T(8,128)(2,1)} %copy.62), calls=%async_computation.1 | async-start | bytes 3211264 | tf_op jit(solution)/shard_map/all_to_all | solution.py:97
  131.2 55.9 %reduce-scatter.2.cloned.1.call-done = f32[384,800]{0,1:T(8,128)} async-done(((f32[3072,800]{0,1:T(8,128)}), f32[384,800]{0,1:T(8,128)}) %reduce-scatter.2.cloned.1.call-update) | async-done | bytes 1228816 | tf_op jit(solution)/shard_map/reduce_scatter | solution.py:99
  187.2 1.4 convert.6
  188.6 1.2 fusion.13
  190.1 1.8 bitcast_reduce_fusion
  192.1 0.5 fusion.43
  192.9 0.6 fusion.1
  194.0 3.0 %fusion.7 = f32[8,48,1,224]{3,1,0,2:T(8,128)S(1)} fusion(f32[8,48]{1,0:T(8,128)S(1)} %add_add_fusion, f32[8,48]{1,0:T(8,128)S(1)} %maximum_maximum_fusion, f32[8,48,2048]{2,1,0:T(8,128)} %copy-done.2, bf16[1,224,2048]{2,1,0:T(8,128)(2,1)} %param.20), kind=kOutput, calls=%fused_computation.14 | convolution fusion | flops 354680832 | bytes 4410368 | tf_op jit(solution)/shard_map/rnhp,hep->rnhe/dot_general | solution.py:67
  197.0 0.7 fusion.12
  197.9 15.2 %all_gather.10 = bf16[384,896]{0,1:T(8,128)(2,1)} all-gather(bf16[384,224]{0,1:T(8,128)(2,1)S(1)} %copy.59), channel_id=1, replica_groups=mesh['gx'=8,'gyx'=4,'gyz'=8] {'gyx'}, dimensions={1}, use_global_device_ids=true | all-gather | bytes 860160 | tf_op jit(solution)/shard_map/all_gather | solution.py:131
  213.1 2.6 %convolution_convert_fusion = bf16[384,896]{1,0:T(8,128)(2,1)S(1)} fusion(bf16[384,896]{0,1:T(8,128)(2,1)} %all_gather.10, bf16[896,896]{1,0:T(8,128)(2,1)} %bitcast.32), kind=kOutput, calls=%fused_computation.9 | convolution fusion | flops 616906752 | bytes 2981888 | tf_op jit(solution)/shard_map/dot_general | solution.py:132
  216.1 27.2 %all_to_all.24 = bf16[384,8,112]{0,2,1:T(8,128)(2,1)S(1)} all-to-all(bf16[384,8,112]{0,2,1:T(8,128)(2,1)S(1)} %bitcast.119), channel_id=1, replica_groups=mesh['gx'=8,'gyx'=4,'gyz'=8] {'gyz'}, dimensions={1} | all-to-all | bytes 1376256 | tf_op jit(solution)/shard_map/all_to_all | solution.py:135
  243.2 0.7 reduce_sum.42
  (45 shorter events, 4.0 us)
Async XLA Ops:
  6.5 185.6 %copy-start = (bf16[8,224,512]{2,1,0:T(8,128)(2,1)S(1)}, bf16[8,224,512]{2,1,0:T(8,128)(2,1)}, u32[]{:S(2)}) copy-start(bf16[8,224,512]{2,1,0:T(8,128)(2,1)} %param.21) | copy-start | bytes 5505028
  6.5 91.9 %all-gather.3.cloned.1.call-start = ((), (), s32[]{:S(2)}) async-start(), calls=%async_computation.3 | async-start | bytes 5677056 | tf_op jit(solution)/shard_map/all_gather | solution.py:98
  7.3 115.9 %all-gather.5.cloned.1.call-start = ((), (), s32[]{:S(2)}) async-start(), calls=%async_computation.5 | async-start | bytes 2064384 | tf_op jit(solution)/shard_map/all_gather | solution.py:96
  9.1 93.9 %copy-start.3 = (bf16[224,896]{1,0:T(8,128)(2,1)S(1)}, bf16[224,896]{1,0:T(8,128)(2,1)}, u32[]{:S(2)}) copy-start(bf16[224,896]{1,0:T(8,128)(2,1)} %param.14) | copy-start | bytes 1204228
  9.1 178.1 %reduce-scatter.2.cloned.1.call-start = ((), (), s32[]{:S(2)}) async-start(), calls=%async_computation.4 | async-start | bytes 11059200 | tf_op jit(solution)/shard_map/reduce_scatter | solution.py:99
  98.5 4.6 %copy-start.1 = (bf16[3072,896]{1,0:T(8,128)(2,1)S(1)}, bf16[3072,896]{1,0:T(8,128)(2,1)}, u32[]{:S(2)}) copy-start(bf16[3072,896]{1,0:T(8,128)(2,1)} %all-gather.3.cloned.1.call-done) | copy-start | bytes 16515076
  103.1 1.9 copy-start.4
  105.0 1.9 copy-start.5
  112.8 0.7 copy-start.9
  112.8 2.7 %copy-start.7 = (s32[8]{0:T(128)S(1)}, s32[8]{0:T(128)}, u32[]{:S(2)}) copy-start(s32[8]{0:T(128)} %param.23) | copy-start | bytes 100
  126.7 61.9 %copy-start.6 = (bf16[224,128]{1,0:T(8,128)(2,1)S(1)}, bf16[224,128]{1,0:T(8,128)(2,1)}, u32[]{:S(2)}) copy-start(bf16[224,128]{1,0:T(8,128)(2,1)} %param.18) | copy-start | bytes 172036
  126.7 86.4 %all-to-all-start = ((bf16[224,4,896]{2,0,1:T(8,128)(2,1)}), bf16[224,4,896]{2,0,1:T(8,128)(2,1)}, u32[]{:S(2)}, u32[]{:S(2)}) async-start(bf16[224,4,896]{2,0,1:T(8,128)(2,1)} %copy.62), calls=%async_computation.1 | async-start | bytes 3211264 | tf_op jit(solution)/shard_map/all_to_all | solution.py:97
  191.9 1.7 copy-start.2
  194.0 3.0 %copy-start.8 = (bf16[8,224,512]{2,1,0:T(8,128)(2,1)S(1)}, bf16[8,224,512]{2,1,0:T(8,128)(2,1)}, u32[]{:S(2)}) copy-start(bf16[8,224,512]{2,1,0:T(8,128)(2,1)} %param.22) | copy-start | bytes 5505028
Sparse Core Ops, SparseCore 0:
  9.9 88.5 all-gather.2
  100.3 22.7 all-gather.4
  125.7 61.4 reduce-scatter.1

commit v2 on v1

--- a/solution.py
+++ b/solution.py
@@ -74,6 +74,15 @@
     return result.astype(jnp.bfloat16)
 
 
+CHUNKS = 1
+
+
+def gather_like_all_to_all(block, axis_name):
+    count = lax.psum(1, axis_name)
+    copies = jnp.broadcast_to(block[None], (count,) + block.shape)
+    return lax.all_to_all(copies, axis_name, 0, 0, tiled=True)
+
+
 def per_device(
     inputs,
     query_weight,
@@ -89,51 +98,59 @@
     parents,
     out_weight,
 ):
-    requests = cache_keys.shape[0]
+    along_x = lax.psum(1, "gyx")
+    along_z = lax.psum(1, "gyz")
+    groups = lax.psum(1, "gx")
     node_count = parents.shape[1]
-    local_rows = requests * node_count
     head_width = query_weight.shape[0]
-    full_columns = lax.all_gather(out_weight, "gx", axis=1, tiled=True)
-    own_block = lax.all_to_all(full_columns, "gyx", 1, 0, tiled=True)
-    all_rows = lax.all_gather(inputs, GY, axis=0, tiled=True)
-    mixture = lax.psum_scatter(
-        jnp.concatenate(
-            [
-                contract_rows(all_rows, matrix)
-                for matrix in (query_weight, key_weight, value_weight, adapter_down)
-            ],
-            axis=1,
-        ),
-        "gx",
-        scatter_dimension=0,
-        tiled=True,
-    )
     head_count = head_width // HEAD
-    query_base = mixture[:, :head_width]
-    new_keys = mixture[:, head_width : 2 * head_width].astype(jnp.bfloat16)
-    new_values = mixture[:, 2 * head_width : 3 * head_width].astype(jnp.bfloat16)
-    adapter_mid = mixture[:, 3 * head_width :].astype(jnp.bfloat16)
-    queries = (query_base + contract_rows(adapter_mid, adapter_up)).astype(jnp.bfloat16)
-    shaped = (requests, node_count, head_count, HEAD)
-    cached = (requests, head_count, HEAD, cache_keys.shape[2])
-    attended = attend(
-        queries.reshape(shaped),
-        new_keys.reshape(shaped),
-        new_values.reshape(shaped),
-        prompt_keys,
-        prompt_values,
-        cache_keys.reshape(cached),
-        cache_values.reshape(cached),
-        cache_lengths,
-        parents,
-    )
-    flattened = attended.reshape(local_rows, head_width)
-    heads_along_x = lax.all_gather(flattened, "gyx", axis=1, tiled=True)
-    partial_sums = jnp.dot(heads_along_x, own_block, preferred_element_type=jnp.float32)
-    parts = lax.psum(1, "gyz")
-    pieces = partial_sums.astype(jnp.bfloat16).reshape(local_rows, parts, -1)
-    arrived = lax.all_to_all(pieces, "gyz", 1, 1, tiled=True)
-    return jnp.sum(arrived.astype(jnp.float32), axis=1).astype(jnp.bfloat16)
+    per_x = groups // along_x
+    columns = out_weight.shape[1]
+    every_block = gather_like_all_to_all(out_weight, "gx")
+    every_block = every_block.reshape(along_x, per_x, head_width, columns)
+    own_block = lax.all_to_all(every_block, "gyx", 0, 0, tiled=True)
+    own_block = own_block.transpose(0, 2, 1, 3).reshape(along_x * head_width, per_x * columns)
+    weights = jnp.concatenate([query_weight, key_weight, value_weight, adapter_down], axis=0)
+    local = inputs.shape[0]
+    rows = local // CHUNKS
+    results = []
+    for chunk in range(CHUNKS):
+        piece = inputs[chunk * rows : (chunk + 1) * rows]
+        gathered = lax.all_gather(lax.all_gather(piece, "gyx", axis=0, tiled=True), "gyz", axis=0, tiled=True)
+        partial = contract_rows(gathered, weights).astype(jnp.bfloat16)
+        per_group_z = along_z * along_x // groups
+        partial = partial.reshape(groups // along_x, per_group_z, along_x, rows, -1)
+        partial = partial.transpose(2, 0, 1, 3, 4).reshape(groups, per_group_z * rows, -1)
+        arrived = lax.all_to_all(partial, "gx", 0, 0, tiled=True)
+        mixture = jnp.sum(arrived.astype(jnp.float32), axis=0)
+        query_base = mixture[:, :head_width]
+        new_keys = mixture[:, head_width : 2 * head_width].astype(jnp.bfloat16)
+        new_values = mixture[:, 2 * head_width : 3 * head_width].astype(jnp.bfloat16)
+        adapter_mid = mixture[:, 3 * head_width :].astype(jnp.bfloat16)
+        queries = (query_base + contract_rows(adapter_mid, adapter_up)).astype(jnp.bfloat16)
+        requests = mixture.shape[0] // node_count
+        shaped = (requests, node_count, head_count, HEAD)
+        cached = (requests, head_count, HEAD, cache_keys.shape[2])
+        attended = attend(
+            queries.reshape(shaped),
+            new_keys.reshape(shaped),
+            new_values.reshape(shaped),
+            prompt_keys,
+            prompt_values,
+            cache_keys[chunk::CHUNKS].reshape(cached),
+            cache_values[chunk::CHUNKS].reshape(cached),
+            cache_lengths[chunk::CHUNKS],
+            parents[chunk::CHUNKS],
+        )
+        flattened = attended.reshape(requests * node_count, head_width)
+        heads_along_x = lax.all_gather(flattened, "gyx", axis=1, tiled=True)
+        partial_sums = jnp.dot(heads_along_x, own_block, preferred_element_type=jnp.float32)
+        pieces = partial_sums.astype(jnp.bfloat16).reshape(requests * node_count, along_z, -1)
+        landed = lax.all_to_all(pieces, "gyz", 1, 1, tiled=True)
+        out = jnp.sum(landed.astype(jnp.float32), axis=1).astype(jnp.bfloat16)
+        results.append(out.reshape(requests, node_count, -1))
+    stacked = jnp.stack(results, axis=1)
+    return stacked.reshape(-1, stacked.shape[-1])
 
 
 def split_mesh(mesh):

time: 251 us -> 253 us (level)
  waiting for transfers between devices: 154 us -> 79 us
  blocking collectives: 42.4 us -> 80.9 us
  local copies, waits for them, and re-layouts: 7.09 us -> 41.9 us
  starting transfers between devices: 4.58 us -> 9.6 us
  matrix products: 22.5 us -> 19.7 us
    all_gather x2 -> x1, waiting for transfers between devices: 96.9 us -> 34.9 us  [per_device(): lax.all_gather(lax.all_gather(piece, 'gyx', axis=0, tiled=True), 'gyz', a...]
    reduce_scatter x1 -> x0, waiting for transfers between devices: 55.9 us -> none  [per_device(): lax.psum_scatter(jnp.concatenate([contract_rows(all_rows, matrix) for mat...]
    all_to_all x1 -> x2, waiting for transfers between devices: 0.01 us -> 44.1 us  [the longest x1 44.1 us: per_device(): arrived = lax.all_to_all(partial, 'gx', 0, 0, tiled=True)]
    all_to_all x1 -> x2, blocking collectives: 27.2 us -> 51.7 us  [the longest x1 28.1 us: gather_like_all_to_all(): return lax.all_to_all(copies, axis_name, 0, 0, tiled=True)]
    all_gather x0 -> x1, blocking collectives: none -> 15.5 us  [per_device(): lax.all_gather(piece, 'gyx', axis=0, tiled=True)]
    reshape x1 -> x3, local copies, waits for them, and re-layouts: 0.15 us -> 15 us  [the longest x1 8.11 us: per_device(): partial.transpose(2, 0, 1, 3, 4).reshape(groups, per_group_z * rows, -1)]
    transpose x0 -> x2, local copies, waits for them, and re-layouts: none -> 10.3 us  [the longest x1 5.63 us: per_device(): partial.transpose(2, 0, 1, 3, 4).reshape(groups, per_group_z * rows, -1)]
    convert_element_type x1 -> x2, local copies, waits for them, and re-layouts: 0.36 us -> 9.13 us  [the longest x1 7.68 us: per_device(): partial = contract_rows(gathered, weights).astype(jnp.bfloat16)]
  transfers between devices with their start and end apart: 4 -> 3, of which waited for: 3 -> 2; matrix products, arithmetic and copies ran while one was open for 13% -> 18% of each run, Pallas kernels for 0% -> 0%
where the time goes in v2:
time: 253 us; the launch traced here: 252 us
  blocking collectives  80.9 us (32%)
  waiting for transfers between devices  79 us (31%)
  local copies, waits for them, and re-layouts  41.9 us (17%)
  matrix products  19.7 us (8%)
  between operations  13.6 us (5%)
  starting transfers between devices  9.6 us (4%)
  other arithmetic  6.84 us (3%)
    all_to_all x1, waiting for transfers between devices, per_device(): arrived = lax.all_to_all(partial, 'gx', 0, 0, tiled=True)  44.1 us
    all_gather x1, waiting for transfers between devices, per_device(): lax.all_gather(lax.all_gather(piece, 'gyx', axis=0, tiled=True), 'gyz', a...  34.9 us
    all_to_all x1, blocking collectives, gather_like_all_to_all(): return lax.all_to_all(copies, axis_name, 0, 0, tiled=True)  28.1 us
    all_to_all x1, blocking collectives, per_device(): landed = lax.all_to_all(pieces, 'gyz', 1, 1, tiled=True)  23.7 us
    all_gather x1, blocking collectives, per_device(): lax.all_gather(piece, 'gyx', axis=0, tiled=True)  15.5 us
    all_gather x1, blocking collectives, per_device(): heads_along_x = lax.all_gather(flattened, 'gyx', axis=1, tiled=True)  13.6 us
    dot_general x2, matrix products, contract_rows(): lax.dot_general(left, right, (((1,), (1,)), ((), ())), preferred_element_...  12.1 us
    reshape x1, local copies, waits for them, and re-layouts, per_device(): partial.transpose(2, 0, 1, 3, 4).reshape(groups, per_group_z * rows, -1)  8.11 us
  transfers between devices with their start and end apart: 3, of which 2 were waited for; matrix products, arithmetic and copies ran while one was open for 18% of the time, Pallas kernels for 0%

profile of v2, /device:TPU:8, one launch (start us, length us, event | category | flops | bytes accessed | tf_op | source)
XLA Modules:
  0.0 251.6 jit_solution(12829747048203918898)
XLA Ops:
  6.5 15.5 %all_gather.9 = bf16[384,896]{1,0:T(8,128)(2,1)} all-gather(bf16[96,896]{1,0:T(8,128)(2,1)} %param.13), channel_id=1, replica_groups=mesh['gx'=8,'gyx'=4,'gyz'=8] {'gyx'}, dimensions={0}, use_global_device_ids=true | all-gather | bytes 860160 | tf_op jit(solution)/shard_map/all_gather | solution.py:119
  22.1 1.1 broadcast_in_dim.21
  23.2 28.1 %all_to_all.20 = bf16[8,224,448]{2,1,0:T(8,128)(2,1)} all-to-all(bf16[8,224,448]{2,1,0:T(8,128)(2,1)S(1)} %broadcast_in_dim.21), channel_id=1, replica_groups=mesh['gx'=8,'gyx'=4,'gyz'=8] {'gx'}, dimensions={0} | all-to-all | bytes 3211264 | tf_op jit(solution)/shard_map/all_to_all | solution.py:83
  51.3 4.4 %all-to-all-start.2 = ((bf16[4,2,224,448]{3,2,1,0:T(8,128)(2,1)}), bf16[4,2,224,448]{3,2,1,0:T(8,128)(2,1)}, u32[]{:S(2)}, u32[]{:S(2)}) async-start(bf16[4,2,224,448]{3,2,1,0:T(8,128)(2,1)} %bitcast.115), calls=%async_computation.2 | async-start | bytes 3670016 | tf_op jit(solution)/shard_map/all_to_all | solution.py:111
  55.7 34.9 %all-gather.2.cloned.1.call-done = bf16[3072,896]{1,0:T(8,128)(2,1)} async-done(((bf16[384,896]{1,0:T(8,128)(2,1)}), bf16[3072,896]{1,0:T(8,128)(2,1)}) %all-gather.2.cloned.1.call-update) | async-done | bytes 5505040 | tf_op jit(solution)/shard_map/all_gather | solution.py:119
  90.6 10.9 %fusion = bf16[3072,800]{0,1:T(8,128)(2,1)} fusion(bf16[3072,896]{1,0:T(8,128)(2,1)} %all-gather.2.cloned.1.call-done, bf16[128,896]{1,0:T(8,128)(2,1)S(1)} %copy-done.10, bf16[224,896]{1,0:T(8,128)(2,1)S(1)} %copy-done.7, bf16[224,896]{1,0:T(8,128)(2,1)S(1)} %copy-done.8, bf16[224,896]{1,0:T(8,128)(2,1)S(1)} %copy-done.9), kind=kOutput, calls=%fused_computation.2 | convolution fusion | flops 4412211200 | bytes 11853824 | tf_op jit(solution)/shard_map/dot_general | solution.py:15
  101.5 7.7 %copy.53 = bf16[3072,800]{1,0:T(8,128)(2,1)} copy(bf16[3072,800]{0,1:T(8,128)(2,1)} %fusion) | data formatting | bytes 9830400 | tf_op jit(solution)/shard_map/convert_element_type | solution.py:120
  109.2 5.6 %copy.54 = bf16[4,2,4,96,800]{4,3,2,1,0:T(8,128)(2,1)} copy(bf16[4,2,4,96,800]{4,3,0,2,1:T(8,128)(2,1)} %bitcast.113) | data formatting | bytes 9830400 | tf_op jit(solution)/shard_map/transpose | solution.py:123
  114.9 8.1 %copy.55 = bf16[8,384,800]{1,2,0:T(8,128)(2,1)} copy(bf16[8,384,800]{2,1,0:T(8,128)(2,1)} %bitcast.114) | data formatting | bytes 9830400 | tf_op jit(solution)/shard_map/reshape | solution.py:123
  123.0 5.2 %all-to-all-start = ((bf16[8,384,800]{1,2,0:T(8,128)(2,1)}), bf16[8,384,800]{1,2,0:T(8,128)(2,1)}, u32[]{:S(2)}, u32[]{:S(2)}) async-start(bf16[8,384,800]{1,2,0:T(8,128)(2,1)} %copy.55), calls=%async_computation | async-start | bytes 9830400 | tf_op jit(solution)/shard_map/all_to_all | solution.py:124
  130.2 4.7 %copy.67 = bf16[4,224,2,448]{3,2,1,0:T(2,128)(2,1)} copy(bf16[4,224,2,448]{3,1,2,0:T(8,128)(2,1)} %bitcast.35) | data formatting | bytes 3211264 | tf_op jit(solution)/shard_map/transpose | solution.py:112
  134.9 5.2 %reshape.162 = bf16[896,896]{1,0:T(8,128)(2,1)} reshape(bf16[4,224,2,448]{3,2,1,0:T(2,128)(2,1)} %copy.67) | data formatting | bytes 3211264 | tf_op jit(solution)/shard_map/reshape | solution.py:112
  140.1 44.1 %all-to-all-done = bf16[8,384,800]{1,2,0:T(8,128)(2,1)} async-done(((bf16[8,384,800]{1,2,0:T(8,128)(2,1)}), bf16[8,384,800]{1,2,0:T(8,128)(2,1)}, u32[]{:S(2)}, u32[]{:S(2)}) %all-to-all-start) | async-done | bytes 4915232 | tf_op jit(solution)/shard_map/all_to_all | solution.py:124
  184.2 4.2 %convert_reduce_fusion = f32[384,800]{0,1:T(8,128)} fusion(bf16[8,384,800]{1,2,0:T(8,128)(2,1)} %all-to-all-done), kind=kLoop, calls=%fused_computation | loop fusion | flops 4608000 | bytes 6144000 | tf_op jit(solution)/shard_map/reduce_sum | solution.py:125
  188.4 1.7 copy.76
  191.8 1.2 copy.77
  193.1 1.9 fusion.50
  195.0 1.2 fusion.21
  200.3 1.4 fusion.20
  201.7 1.7 copy.66
  203.4 13.6 %all_gather.11 = bf16[384,896]{0,1:T(8,128)(2,1)S(1)} all-gather(bf16[384,224]{0,1:T(8,128)(2,1)} %copy.66), channel_id=1, replica_groups=mesh['gx'=8,'gyx'=4,'gyz'=8] {'gyx'}, dimensions={1}, use_global_device_ids=true | all-gather | bytes 860160 | tf_op jit(solution)/shard_map/all_gather | solution.py:146
  217.0 1.8 convolution_convert_fusion.1
  218.9 1.4 copy.68
  220.3 23.7 %all_to_all.21 = bf16[384,8,112]{0,2,1:T(8,128)(2,1)S(1)} all-to-all(bf16[384,8,112]{0,2,1:T(8,128)(2,1)S(1)} %bitcast.119), channel_id=1, replica_groups=mesh['gx'=8,'gyx'=4,'gyz'=8] {'gyz'}, dimensions={1} | all-to-all | bytes 1376256 | tf_op jit(solution)/shard_map/all_to_all | solution.py:149
  (49 shorter events, 8.5 us)
Async XLA Ops:
  6.5 190.7 %copy-start = (bf16[8,224,512]{2,1,0:T(8,128)(2,1)S(1)}, bf16[8,224,512]{2,1,0:T(8,128)(2,1)}, u32[]{:S(2)}) copy-start(bf16[8,224,512]{2,1,0:T(8,128)(2,1)} %param.21) | copy-start | bytes 5505028
  6.5 84.1 %all-gather.2.cloned.1.call-start = ((), (), s32[]{:S(2)}) async-start(), calls=%async_computation.4 | async-start | bytes 6193152 | tf_op jit(solution)/shard_map/all_gather | solution.py:119
  23.2 67.4 %copy-start.7 = (bf16[224,896]{1,0:T(8,128)(2,1)S(1)}, bf16[224,896]{1,0:T(8,128)(2,1)}, u32[]{:S(2)}) copy-start(bf16[224,896]{1,0:T(8,128)(2,1)} %param.16) | copy-start | bytes 1204228
  23.2 67.4 %copy-start.8 = (bf16[224,896]{1,0:T(8,128)(2,1)S(1)}, bf16[224,896]{1,0:T(8,128)(2,1)}, u32[]{:S(2)}) copy-start(bf16[224,896]{1,0:T(8,128)(2,1)} %param.15) | copy-start | bytes 1204228
  23.2 67.4 %copy-start.9 = (bf16[224,896]{1,0:T(8,128)(2,1)S(1)}, bf16[224,896]{1,0:T(8,128)(2,1)}, u32[]{:S(2)}) copy-start(bf16[224,896]{1,0:T(8,128)(2,1)} %param.14) | copy-start | bytes 1204228
  23.2 67.4 %copy-start.10 = (bf16[128,896]{1,0:T(8,128)(2,1)S(1)}, bf16[128,896]{1,0:T(8,128)(2,1)}, u32[]{:S(2)}) copy-start(bf16[128,896]{1,0:T(8,128)(2,1)} %param.17) | copy-start | bytes 688132
  51.3 71.6 %all-to-all-start.2 = ((bf16[4,2,224,448]{3,2,1,0:T(8,128)(2,1)}), bf16[4,2,224,448]{3,2,1,0:T(8,128)(2,1)}, u32[]{:S(2)}, u32[]{:S(2)}) async-start(bf16[4,2,224,448]{3,2,1,0:T(8,128)(2,1)} %bitcast.115), calls=%async_computation.2 | async-start | bytes 3670016 | tf_op jit(solution)/shard_map/all_to_all | solution.py:111
  123.0 5.2 %copy-start.11 = (s32[8,48]{1,0:T(8,128)S(1)}, s32[8,48]{1,0:T(8,128)}, u32[]{:S(2)}) copy-start(s32[8,48]{1,0:T(8,128)} %param.24) | copy-start | bytes 4612
  123.0 61.2 %all-to-all-start = ((bf16[8,384,800]{1,2,0:T(8,128)(2,1)}), bf16[8,384,800]{1,2,0:T(8,128)(2,1)}, u32[]{:S(2)}, u32[]{:S(2)}) async-start(bf16[8,384,800]{1,2,0:T(8,128)(2,1)} %copy.55), calls=%async_computation | async-start | bytes 9830400 | tf_op jit(solution)/shard_map/all_to_all | solution.py:124
  128.2 2.0 copy-start.4
  191.8 4.5 %copy-start.2 = (bf16[1,224,2048]{2,1,0:T(8,128)(2,1)S(1)}, bf16[1,224,2048]{2,1,0:T(8,128)(2,1)}, u32[]{:S(2)}) copy-start(bf16[1,224,2048]{2,1,0:T(8,128)(2,1)} %param.19) | copy-start | bytes 2752516
  197.2 1.4 copy-start.6
  198.7 0.9 copy-start.3
  198.7 1.6 copy-start.5
  200.3 16.7 %copy-start.1 = (bf16[896,896]{1,0:T(8,128)(2,1)S(1)}, bf16[896,896]{1,0:T(8,128)(2,1)}, u32[]{:S(2)}) copy-start(bf16[896,896]{1,0:T(8,128)(2,1)} %reshape.162) | copy-start | bytes 4816900
Sparse Core Ops, SparseCore 0:
  22.2 68.3 all-gather.1

commit v3 on v2

--- a/solution.py
+++ b/solution.py
@@ -116,13 +116,9 @@
     results = []
     for chunk in range(CHUNKS):
         piece = inputs[chunk * rows : (chunk + 1) * rows]
-        gathered = lax.all_gather(lax.all_gather(piece, "gyx", axis=0, tiled=True), "gyz", axis=0, tiled=True)
+        gathered = lax.all_gather(piece, GY, axis=0, tiled=True)
         partial = contract_rows(gathered, weights).astype(jnp.bfloat16)
-        per_group_z = along_z * along_x // groups
-        partial = partial.reshape(groups // along_x, per_group_z, along_x, rows, -1)
-        partial = partial.transpose(2, 0, 1, 3, 4).reshape(groups, per_group_z * rows, -1)
-        arrived = lax.all_to_all(partial, "gx", 0, 0, tiled=True)
-        mixture = jnp.sum(arrived.astype(jnp.float32), axis=0)
+        mixture = lax.psum_scatter(partial, "gx", scatter_dimension=0, tiled=True).astype(jnp.float32)
         query_base = mixture[:, :head_width]
         new_keys = mixture[:, head_width : 2 * head_width].astype(jnp.bfloat16)
         new_values = mixture[:, 2 * head_width : 3 * head_width].astype(jnp.bfloat16)

time: 253 us -> 249 us (0.984)
  waiting for transfers between devices: 79 us -> 146 us
  blocking collectives: 80.9 us -> 34.4 us
  local copies, waits for them, and re-layouts: 41.9 us -> 26.1 us
  other arithmetic: 6.84 us -> 1.7 us
    all_gather x1, waiting for transfers between devices: 34.9 us -> 91.2 us  [per_device(): gathered = lax.all_gather(piece, GY, axis=0, tiled=True)]
    all_to_all x1 -> x0, blocking collectives: 28.1 us -> none  [gather_like_all_to_all(): return lax.all_to_all(copies, axis_name, 0, 0, tiled=True)]
    all_to_all x1, waiting for transfers between devices: 0.01 us -> 21.3 us  [per_device(): own_block = lax.all_to_all(every_block, 'gyx', 0, 0, tiled=True)]
    all_gather x1 -> x0, blocking collectives: 15.5 us -> none  [per_device(): lax.all_gather(piece, 'gyx', axis=0, tiled=True)]
    all_to_all x1, waiting for transfers between devices: 44.1 us -> 32.4 us  [gather_like_all_to_all(): return lax.all_to_all(copies, axis_name, 0, 0, tiled=True)]
    reshape x1 -> x0, local copies, waits for them, and re-layouts: 8.11 us -> none  [per_device(): partial.transpose(2, 0, 1, 3, 4).reshape(groups, per_group_z * rows, -1)]
    convert_element_type x1 -> x0, local copies, waits for them, and re-layouts: 7.68 us -> none  [per_device(): partial = contract_rows(gathered, weights).astype(jnp.bfloat16)]
    unnamed x26 -> x20, local copies, waits for them, and re-layouts: 3.6 us -> 9.36 us
  transfers between devices with their start and end apart: 3 -> 4, of which waited for: 2 -> 3; matrix products, arithmetic and copies ran while one was open for 18% -> 5% of each run, Pallas kernels for 0% -> 0%
where the time goes in v3:
time: 249 us
  waiting for transfers between devices  146 us (59%)
  blocking collectives  34.4 us (14%)
  local copies, waits for them, and re-layouts  26.1 us (10%)
  matrix products  18 us (7%)
  between operations  13.6 us (5%)
  starting transfers between devices  9.39 us (4%)
    all_gather x1, waiting for transfers between devices, per_device(): gathered = lax.all_gather(piece, GY, axis=0, tiled=True)  91.2 us
    all_to_all x1, waiting for transfers between devices, gather_like_all_to_all(): return lax.all_to_all(copies, axis_name, 0, 0, tiled=True)  32.4 us
    all_to_all x1, waiting for transfers between devices, per_device(): own_block = lax.all_to_all(every_block, 'gyx', 0, 0, tiled=True)  21.3 us
    all_to_all x1, blocking collectives, per_device(): landed = lax.all_to_all(pieces, 'gyz', 1, 1, tiled=True)  20.9 us
    all_gather x1, blocking collectives, per_device(): heads_along_x = lax.all_gather(flattened, 'gyx', axis=1, tiled=True)  13.4 us
    dot_general x2, matrix products, contract_rows(): lax.dot_general(left, right, (((1,), (1,)), ((), ())), preferred_element_...  10.5 us
    unnamed x20, local copies, waits for them, and re-layouts  9.36 us
    reshape x1, local copies, waits for them, and re-layouts, per_device(): own_block.transpose(0, 2, 1, 3)  5.27 us
  transfers between devices with their start and end apart: 4, of which 3 were waited for; matrix products, arithmetic and copies ran while one was open for 5% of the time, Pallas kernels for 0%

profile of v3, /device:TPU:8, one launch (start us, length us, event | category | flops | bytes accessed | tf_op | source)
XLA Modules:
  0.0 248.7 jit_solution(9943479394391978656)
XLA Ops:
  6.5 0.7 all-gather.2.cloned.1.call-update
  7.3 91.2 %all-gather.2.cloned.1.call-done = bf16[3072,896]{1,0:T(8,128)(2,1)} async-done(((bf16[96,896]{1,0:T(8,128)(2,1)}), bf16[3072,896]{1,0:T(8,128)(2,1)}) %all-gather.2.cloned.1.call-update) | async-done | bytes 5505040 | tf_op jit(solution)/shard_map/all_gather | solution.py:119
  98.5 9.2 %fusion = bf16[3072,800]{0,1:T(8,128)(2,1)} fusion(bf16[3072,896]{1,0:T(8,128)(2,1)} %all-gather.2.cloned.1.call-done, bf16[128,896]{1,0:T(8,128)(2,1)} %param.17, bf16[224,896]{1,0:T(8,128)(2,1)} %param.16, bf16[224,896]{1,0:T(8,128)(2,1)} %param.15, bf16[224,896]{1,0:T(8,128)(2,1)} %param.14), kind=kOutput, calls=%fused_computation.1 | convolution fusion | flops 4412211200 | bytes 11853824 | tf_op jit(solution)/shard_map/dot_general | solution.py:15
  107.7 7.7 %copy.69 = bf16[3072,800]{1,0:T(8,128)(2,1)} copy(bf16[3072,800]{0,1:T(8,128)(2,1)} %fusion) | data formatting | bytes 9830400
  115.4 0.9 copy-done.3
  116.3 1.5 broadcast_in_dim.21
  117.8 4.8 %all-to-all-start = ((bf16[8,224,448]{2,1,0:T(8,128)(2,1)}), bf16[8,224,448]{2,1,0:T(8,128)(2,1)}, u32[]{:S(2)}, u32[]{:S(2)}) async-start(bf16[8,224,448]{2,1,0:T(8,128)(2,1)} %broadcast_in_dim.21), calls=%async_computation | async-start | bytes 3670016 | tf_op jit(solution)/shard_map/all_to_all | solution.py:83
  123.0 32.4 %all-to-all-done = bf16[8,224,448]{2,1,0:T(8,128)(2,1)} async-done(((bf16[8,224,448]{2,1,0:T(8,128)(2,1)}), bf16[8,224,448]{2,1,0:T(8,128)(2,1)}, u32[]{:S(2)}, u32[]{:S(2)}) %all-to-all-start) | async-done | bytes 1605664 | tf_op jit(solution)/shard_map/all_to_all | solution.py:83
  155.4 4.5 %all-to-all-start.1 = ((bf16[4,2,224,448]{3,2,1,0:T(8,128)(2,1)}), bf16[4,2,224,448]{3,2,1,0:T(8,128)(2,1)}, u32[]{:S(2)}, u32[]{:S(2)}) async-start(bf16[4,2,224,448]{3,2,1,0:T(8,128)(2,1)} %bitcast.31), calls=%async_computation.1 | async-start | bytes 3670016 | tf_op jit(solution)/shard_map/all_to_all | solution.py:111
  161.6 21.3 %all-to-all-done.1 = bf16[4,2,224,448]{3,2,1,0:T(8,128)(2,1)} async-done(((bf16[4,2,224,448]{3,2,1,0:T(8,128)(2,1)}), bf16[4,2,224,448]{3,2,1,0:T(8,128)(2,1)}, u32[]{:S(2)}, u32[]{:S(2)}) %all-to-all-start.1) | async-done | bytes 1605664 | tf_op jit(solution)/shard_map/all_to_all | solution.py:111
  182.9 4.7 %copy.60 = bf16[4,224,2,448]{3,2,1,0:T(2,128)(2,1)} copy(bf16[4,224,2,448]{3,1,2,0:T(8,128)(2,1)} %bitcast.32) | data formatting | bytes 3211264 | tf_op jit(solution)/shard_map/transpose | solution.py:112
  187.6 5.3 %reshape.154 = bf16[896,896]{1,0:T(8,128)(2,1)} reshape(bf16[4,224,2,448]{3,2,1,0:T(2,128)(2,1)} %copy.60) | data formatting | bytes 3211264 | tf_op jit(solution)/shard_map/reshape | solution.py:112
  192.8 2.0 fusion.50
  195.0 1.2 fusion.21
  196.4 0.7 bitcast_reduce_fusion
  198.2 0.6 fusion.2
  198.8 0.7 fusion.15
  200.4 1.4 fusion.20
  201.8 1.7 copy.59
  203.5 13.4 %all_gather.7 = bf16[384,896]{0,1:T(8,128)(2,1)S(1)} all-gather(bf16[384,224]{0,1:T(8,128)(2,1)} %copy.59), channel_id=1, replica_groups=mesh['gx'=8,'gyx'=4,'gyz'=8] {'gyx'}, dimensions={1}, use_global_device_ids=true | all-gather | bytes 860160 | tf_op jit(solution)/shard_map/all_gather | solution.py:142
  216.9 1.8 convolution_convert_fusion.1
  218.7 1.4 copy.61
  220.2 20.9 %all_to_all.15 = bf16[384,8,112]{0,2,1:T(8,128)(2,1)S(1)} all-to-all(bf16[384,8,112]{0,2,1:T(8,128)(2,1)S(1)} %bitcast.113), channel_id=1, replica_groups=mesh['gx'=8,'gyx'=4,'gyz'=8] {'gyz'}, dimensions={1} | all-to-all | bytes 1376256 | tf_op jit(solution)/shard_map/all_to_all | solution.py:145
  241.1 0.7 reduce_sum.42
  (38 shorter events, 4.3 us)
Async XLA Ops:
  6.5 190.8 %copy-start = (bf16[8,224,512]{2,1,0:T(8,128)(2,1)S(1)}, bf16[8,224,512]{2,1,0:T(8,128)(2,1)}, u32[]{:S(2)}) copy-start(bf16[8,224,512]{2,1,0:T(8,128)(2,1)} %param.21) | copy-start | bytes 5505028
  6.5 91.9 %all-gather.2.cloned.1.call-start = ((), (), s32[]{:S(2)}) async-start(), calls=%async_computation.4 | async-start | bytes 5677056 | tf_op jit(solution)/shard_map/all_gather | solution.py:119
  7.3 185.6 %reduce-scatter.4.cloned.1.call-start = ((), (), s32[]{:S(2)}) async-start(), calls=%async_computation.5 | async-start | bytes 6193152 | tf_op jit(solution)/shard_map/reduce_scatter | solution.py:121
  115.4 0.9 copy-start.3
  116.3 6.3 %copy-start.8 = (s32[8,48]{1,0:T(8,128)S(1)}, s32[8,48]{1,0:T(8,128)}, u32[]{:S(2)}) copy-start(s32[8,48]{1,0:T(8,128)} %param.24) | copy-start | bytes 4612
  117.8 37.6 %all-to-all-start = ((bf16[8,224,448]{2,1,0:T(8,128)(2,1)}), bf16[8,224,448]{2,1,0:T(8,128)(2,1)}, u32[]{:S(2)}, u32[]{:S(2)}) async-start(bf16[8,224,448]{2,1,0:T(8,128)(2,1)} %broadcast_in_dim.21), calls=%async_computation | async-start | bytes 3670016 | tf_op jit(solution)/shard_map/all_to_all | solution.py:83
  155.4 6.1 %copy-start.5 = (s32[8]{0:T(128)S(1)}, s32[8]{0:T(128)}, u32[]{:S(2)}) copy-start(s32[8]{0:T(128)} %param.23) | copy-start | bytes 100
  155.4 27.5 %all-to-all-start.1 = ((bf16[4,2,224,448]{3,2,1,0:T(8,128)(2,1)}), bf16[4,2,224,448]{3,2,1,0:T(8,128)(2,1)}, u32[]{:S(2)}, u32[]{:S(2)}) async-start(bf16[4,2,224,448]{3,2,1,0:T(8,128)(2,1)} %bitcast.31), calls=%async_computation.1 | async-start | bytes 3670016 | tf_op jit(solution)/shard_map/all_to_all | solution.py:111
  187.6 8.8 %copy-start.2 = (bf16[1,224,2048]{2,1,0:T(8,128)(2,1)S(1)}, bf16[1,224,2048]{2,1,0:T(8,128)(2,1)}, u32[]{:S(2)}) copy-start(bf16[1,224,2048]{2,1,0:T(8,128)(2,1)} %param.19) | copy-start | bytes 2752516
  197.3 1.4 copy-start.7
  198.8 0.9 copy-start.4
  198.8 1.6 copy-start.6
  200.4 16.5 %copy-start.1 = (bf16[896,896]{1,0:T(8,128)(2,1)S(1)}, bf16[896,896]{1,0:T(8,128)(2,1)}, u32[]{:S(2)}) copy-start(bf16[896,896]{1,0:T(8,128)(2,1)} %reshape.154) | copy-start | bytes 4816900
Sparse Core Ops, SparseCore 0:
  9.9 88.5 all-gather.1
  115.5 55.5 reduce-scatter.3

commit v4 on v3

--- a/solution.py
+++ b/solution.py
@@ -109,16 +109,21 @@
     every_block = gather_like_all_to_all(out_weight, "gx")
     every_block = every_block.reshape(along_x, per_x, head_width, columns)
     own_block = lax.all_to_all(every_block, "gyx", 0, 0, tiled=True)
-    own_block = own_block.transpose(0, 2, 1, 3).reshape(along_x * head_width, per_x * columns)
-    weights = jnp.concatenate([query_weight, key_weight, value_weight, adapter_down], axis=0)
+    weights = (query_weight, key_weight, value_weight, adapter_down)
     local = inputs.shape[0]
     rows = local // CHUNKS
     results = []
     for chunk in range(CHUNKS):
         piece = inputs[chunk * rows : (chunk + 1) * rows]
         gathered = lax.all_gather(piece, GY, axis=0, tiled=True)
-        partial = contract_rows(gathered, weights).astype(jnp.bfloat16)
-        mixture = lax.psum_scatter(partial, "gx", scatter_dimension=0, tiled=True).astype(jnp.float32)
+        if chunk == 0:
+            gathered, own_block = lax.optimization_barrier((gathered, own_block))
+        mixture = lax.psum_scatter(
+            jnp.concatenate([contract_rows(gathered, matrix) for matrix in weights], axis=1),
+            "gx",
+            scatter_dimension=0,
+            tiled=True,
+        )
         query_base = mixture[:, :head_width]
         new_keys = mixture[:, head_width : 2 * head_width].astype(jnp.bfloat16)
         new_values = mixture[:, 2 * head_width : 3 * head_width].astype(jnp.bfloat16)
@@ -140,7 +145,10 @@
         )
         flattened = attended.reshape(requests * node_count, head_width)
         heads_along_x = lax.all_gather(flattened, "gyx", axis=1, tiled=True)
-        partial_sums = jnp.dot(heads_along_x, own_block, preferred_element_type=jnp.float32)
+        heads_along_x = heads_along_x.reshape(requests * node_count, along_x, head_width)
+        partial_sums = jnp.einsum(
+            "txe,xkec->tkc", heads_along_x, own_block, preferred_element_type=jnp.float32
+        )
         pieces = partial_sums.astype(jnp.bfloat16).reshape(requests * node_count, along_z, -1)
         landed = lax.all_to_all(pieces, "gyz", 1, 1, tiled=True)
         out = jnp.sum(landed.astype(jnp.float32), axis=1).astype(jnp.bfloat16)

time: 249 us -> 232 us (0.932)
  blocking collectives: 34.4 us -> 96.9 us
  waiting for transfers between devices: 146 us -> 89.3 us
  local copies, waits for them, and re-layouts: 26.1 us -> 2.47 us
  starting transfers between devices: 9.39 us -> 0.04 us
  other arithmetic: 1.7 us -> 7 us
  matrix products: 18 us -> 22.5 us
    all_gather x1, waiting for transfers between devices: 91.2 us -> 34.6 us  [per_device(): gathered = lax.all_gather(piece, GY, axis=0, tiled=True)]
    all_to_all x0 -> x2, blocking collectives: none -> 55.3 us  [the longest x1 28 us: gather_like_all_to_all(): return lax.all_to_all(copies, axis_name, 0, 0, tiled=True)]
    reduce_scatter x1, waiting for transfers between devices: 0.01 us -> 53.9 us  [per_device(): lax.psum_scatter(jnp.concatenate([contract_rows(gathered, matrix) for mat...]
    all_to_all x2 -> x0, waiting for transfers between devices: 53.7 us -> none  [the longest x1 32.4 us: gather_like_all_to_all(): return lax.all_to_all(copies, axis_name, 0, 0, tiled=True)]
    all_to_all x2 -> x0, starting transfers between devices: 9.35 us -> none  [the longest x1 4.83 us: gather_like_all_to_all(): return lax.all_to_all(copies, axis_name, 0, 0, tiled=True)]
    unnamed x20 -> x22, local copies, waits for them, and re-layouts: 9.36 us -> 0.76 us
    all_to_all x1, blocking collectives: 20.9 us -> 27.2 us  [per_device(): landed = lax.all_to_all(pieces, 'gyz', 1, 1, tiled=True)]
    reshape x1 -> x0, local copies, waits for them, and re-layouts: 5.27 us -> none  [per_device(): own_block.transpose(0, 2, 1, 3)]
  transfers between devices with their start and end apart: 4 -> 2, of which waited for: 3 -> 2; matrix products, arithmetic and copies ran while one was open for 5% -> 1% of each run, Pallas kernels for 0% -> 0%
where the time goes in v4:
time: 232 us
  blocking collectives  96.9 us (42%)
  waiting for transfers between devices  89.3 us (38%)
  matrix products  22.5 us (10%)
  between operations  13.7 us (6%)
  other arithmetic  7 us (3%)
  local copies, waits for them, and re-layouts  2.47 us (1%)
    reduce_scatter x1, waiting for transfers between devices, per_device(): lax.psum_scatter(jnp.concatenate([contract_rows(gathered, matrix) for mat...  53.9 us
    all_gather x1, waiting for transfers between devices, per_device(): gathered = lax.all_gather(piece, GY, axis=0, tiled=True)  34.6 us
    all_to_all x1, blocking collectives, gather_like_all_to_all(): return lax.all_to_all(copies, axis_name, 0, 0, tiled=True)  28 us
    all_to_all x1, blocking collectives, per_device(): own_block = lax.all_to_all(every_block, 'gyx', 0, 0, tiled=True)  27.3 us
    all_to_all x1, blocking collectives, per_device(): landed = lax.all_to_all(pieces, 'gyz', 1, 1, tiled=True)  27.2 us
    all_gather x1, blocking collectives, per_device(): heads_along_x = lax.all_gather(flattened, 'gyx', axis=1, tiled=True)  14.4 us
    dot_general x5, matrix products, contract_rows(): lax.dot_general(left, right, (((1,), (1,)), ((), ())), preferred_element_...  11.4 us
  transfers between devices with their start and end apart: 2, of which 2 were waited for; matrix products, arithmetic and copies ran while one was open for 1% of the time, Pallas kernels for 0%

profile of v4, /device:TPU:8, one launch (start us, length us, event | category | flops | bytes accessed | tf_op | source)
XLA Modules:
  0.0 231.9 jit_solution(2346064940070692924)
XLA Ops:
  6.5 0.7 all-gather.2.cloned.1.call-update
  7.3 1.1 broadcast_in_dim.17
  8.4 28.0 %all_to_all.15 = bf16[8,224,448]{2,1,0:T(8,128)(2,1)S(1)} all-to-all(bf16[8,224,448]{2,1,0:T(8,128)(2,1)S(1)} %broadcast_in_dim.17), channel_id=1, replica_groups=mesh['gx'=8,'gyx'=4,'gyz'=8] {'gx'}, dimensions={0} | all-to-all | bytes 3211264 | tf_op jit(solution)/shard_map/all_to_all | solution.py:83
  36.4 27.3 %all_to_all.16 = bf16[4,2,224,448]{3,2,1,0:T(8,128)(2,1)} all-to-all(bf16[4,2,224,448]{3,2,1,0:T(8,128)(2,1)S(1)} %bitcast.125), channel_id=1, replica_groups=mesh['gx'=8,'gyx'=4,'gyz'=8] {'gyx'}, dimensions={0} | all-to-all | bytes 3211264 | tf_op jit(solution)/shard_map/all_to_all | solution.py:111
  63.7 34.6 %all-gather.2.cloned.1.call-done = bf16[3072,896]{1,0:T(8,128)(2,1)} async-done(((bf16[96,896]{1,0:T(8,128)(2,1)}), bf16[3072,896]{1,0:T(8,128)(2,1)}) %all-gather.2.cloned.1.call-update) | async-done | bytes 5505040 | tf_op jit(solution)/shard_map/all_gather | solution.py:118
  98.4 4.6 %fusion.45 = f32[3072,224]{0,1:T(8,128)S(1)} fusion(bf16[3072,896]{1,0:T(8,128)(2,1)} %all-gather.2.cloned.1.call-done, bf16[224,896]{1,0:T(8,128)(2,1)S(1)} %copy-done.3), kind=kOutput, calls=%fused_computation.69 | convolution fusion | flops 1233125376 | bytes 8658944 | tf_op jit(solution)/shard_map/dot_general | solution.py:15
  103.0 1.9 fusion.46
  105.0 1.9 fusion.47
  106.9 1.9 fusion.48
  108.7 3.9 %pad_maximum_fusion = f32[3072,800]{0,1:T(8,128)} fusion(f32[3072,128]{0,1:T(8,128)S(1)} %fusion.48, f32[3072,224]{0,1:T(8,128)S(1)} %fusion.47, f32[3072,224]{0,1:T(8,128)S(1)} %fusion.46, f32[3072,224]{0,1:T(8,128)S(1)} %fusion.45), kind=kLoop, calls=%fused_computation | loop fusion | flops 7372800 | bytes 19660800 | tf_op jit(solution)/shard_map/concatenate | solution.py:122
  112.7 0.6 copy-done.10
  113.4 0.4 fusion.15
  115.4 53.9 %reduce-scatter.2.cloned.1.call-done = f32[384,800]{0,1:T(8,128)} async-done(((f32[3072,800]{0,1:T(8,128)}), f32[384,800]{0,1:T(8,128)}) %reduce-scatter.2.cloned.1.call-update) | async-done | bytes 1228816 | tf_op jit(solution)/shard_map/reduce_scatter | solution.py:121
  169.4 1.4 convert.6
  170.8 1.2 fusion.14
  172.3 1.8 bitcast_reduce_fusion
  174.3 0.5 fusion.44
  175.1 0.6 fusion.1
  176.0 3.0 %fusion.8 = f32[8,48,1,224]{3,1,0,2:T(8,128)S(1)} fusion(f32[8,48]{1,0:T(8,128)S(1)} %add_add_fusion, f32[8,48]{1,0:T(8,128)S(1)} %maximum_maximum_fusion, f32[8,48,2048]{2,1,0:T(8,128)} %copy-done.2, bf16[1,224,2048]{2,1,0:T(8,128)(2,1)} %param.20), kind=kOutput, calls=%fused_computation.15 | convolution fusion | flops 354680832 | bytes 4410368 | tf_op jit(solution)/shard_map/rnhp,hep->rnhe/dot_general | solution.py:67
  179.2 0.7 fusion.13
  180.1 14.4 %all_gather.7 = bf16[384,896]{0,1:T(8,128)(2,1)S(1)} all-gather(bf16[384,224]{0,1:T(8,128)(2,1)S(1)} %copy.49), channel_id=1, replica_groups=mesh['gx'=8,'gyx'=4,'gyz'=8] {'gyx'}, dimensions={1}, use_global_device_ids=true | all-gather | bytes 860160 | tf_op jit(solution)/shard_map/all_gather | solution.py:147
  194.5 2.6 %fusion.4 = bf16[384,2,448]{0,2,1:T(8,128)(2,1)S(1)} fusion(bf16[384,4,224,1]{0,2,3,1:T(8,128)(2,1)S(1)} %bitcast.131, bf16[4,2,224,448]{3,2,1,0:T(8,128)(2,1)} %all_to_all.16), kind=kOutput, calls=%fused_computation.10 | convolution fusion | flops 616906752 | bytes 2981888 | tf_op jit(solution)/shard_map/txe,xkec->tkc/dot_general | solution.py:149
  197.2 27.2 %all_to_all.17 = bf16[384,8,112]{0,2,1:T(8,128)(2,1)S(1)} all-to-all(bf16[384,8,112]{0,2,1:T(8,128)(2,1)S(1)} %bitcast.130), channel_id=1, replica_groups=mesh['gx'=8,'gyx'=4,'gyz'=8] {'gyz'}, dimensions={1} | all-to-all | bytes 1376256 | tf_op jit(solution)/shard_map/all_to_all | solution.py:153
  224.4 0.7 reduce_sum.42
  (42 shorter events, 3.2 us)
Async XLA Ops:
  6.5 167.8 %copy-start = (bf16[8,224,512]{2,1,0:T(8,128)(2,1)S(1)}, bf16[8,224,512]{2,1,0:T(8,128)(2,1)}, u32[]{:S(2)}) copy-start(bf16[8,224,512]{2,1,0:T(8,128)(2,1)} %param.21) | copy-start | bytes 5505028
  6.5 91.8 %all-gather.2.cloned.1.call-start = ((), (), s32[]{:S(2)}) async-start(), calls=%async_computation.4 | async-start | bytes 5677056 | tf_op jit(solution)/shard_map/all_gather | solution.py:118
  7.3 162.1 %reduce-scatter.2.cloned.1.call-start = ((), (), s32[]{:S(2)}) async-start(), calls=%async_computation.5 | async-start | bytes 11059200 | tf_op jit(solution)/shard_map/reduce_scatter | solution.py:121
  8.4 90.0 %copy-start.3 = (bf16[224,896]{1,0:T(8,128)(2,1)S(1)}, bf16[224,896]{1,0:T(8,128)(2,1)}, u32[]{:S(2)}) copy-start(bf16[224,896]{1,0:T(8,128)(2,1)} %param.14) | copy-start | bytes 1204228
  63.7 39.3 %copy-start.4 = (bf16[224,896]{1,0:T(8,128)(2,1)S(1)}, bf16[224,896]{1,0:T(8,128)(2,1)}, u32[]{:S(2)}) copy-start(bf16[224,896]{1,0:T(8,128)(2,1)} %param.15) | copy-start | bytes 1204228
  98.4 4.6 %copy-start.1 = (bf16[3072,896]{1,0:T(8,128)(2,1)S(1)}, bf16[3072,896]{1,0:T(8,128)(2,1)}, u32[]{:S(2)}) copy-start(bf16[3072,896]{1,0:T(8,128)(2,1)} %all-gather.2.cloned.1.call-done) | copy-start | bytes 16515076
  103.0 1.9 copy-start.5
  105.0 1.9 copy-start.6
  112.7 0.7 copy-start.10
  112.7 2.7 %copy-start.8 = (s32[8]{0:T(128)S(1)}, s32[8]{0:T(128)}, u32[]{:S(2)}) copy-start(s32[8]{0:T(128)} %param.23) | copy-start | bytes 100
  112.7 58.1 %copy-start.7 = (bf16[224,128]{1,0:T(8,128)(2,1)S(1)}, bf16[224,128]{1,0:T(8,128)(2,1)}, u32[]{:S(2)}) copy-start(bf16[224,128]{1,0:T(8,128)(2,1)} %param.18) | copy-start | bytes 172036
  174.1 1.7 copy-start.2
  176.0 3.2 %copy-start.9 = (bf16[8,224,512]{2,1,0:T(8,128)(2,1)S(1)}, bf16[8,224,512]{2,1,0:T(8,128)(2,1)}, u32[]{:S(2)}) copy-start(bf16[8,224,512]{2,1,0:T(8,128)(2,1)} %param.22) | copy-start | bytes 5505028
Sparse Core Ops, SparseCore 0:
  9.9 88.4 all-gather.1
  112.8 56.4 reduce-scatter.1

commit v5 on v4

--- a/solution.py
+++ b/solution.py
@@ -74,7 +74,7 @@
     return result.astype(jnp.bfloat16)
 
 
-CHUNKS = 1
+CHUNKS = 2
 
 
 def gather_like_all_to_all(block, axis_name):
@@ -116,7 +116,7 @@
     for chunk in range(CHUNKS):
         piece = inputs[chunk * rows : (chunk + 1) * rows]
         gathered = lax.all_gather(piece, GY, axis=0, tiled=True)
-        if chunk == 0:
+        if chunk == CHUNKS - 1:
             gathered, own_block = lax.optimization_barrier((gathered, own_block))
         mixture = lax.psum_scatter(
             jnp.concatenate([contract_rows(gathered, matrix) for matrix in weights], axis=1),

time: 232 us -> 318 us (1.37); the launches traced: 232 us -> 314 us
  waiting for transfers between devices: 89.3 us -> 138 us
  local copies, waits for them, and re-layouts: 2.47 us -> 25.3 us
  starting transfers between devices: 0.04 us -> 14.3 us
  blocking collectives: 96.9 us -> 90.9 us
    all_gather x1 -> x2, waiting for transfers between devices: 34.6 us -> 88.2 us  [per_device(): gathered = lax.all_gather(piece, GY, axis=0, tiled=True)]
    all_to_all x1 -> x0, blocking collectives: 27.2 us -> none  [per_device(): landed = lax.all_to_all(pieces, 'gyz', 1, 1, tiled=True)]
    reduce_scatter x1 -> x2, waiting for transfers between devices: 53.9 us -> 35.9 us  [per_device(): lax.psum_scatter(jnp.concatenate([contract_rows(gathered, matrix) for mat...]
    unnamed x22 -> x42, local copies, waits for them, and re-layouts: 0.76 us -> 16.7 us
    all_to_all x0 -> x2, starting transfers between devices: none -> 14.2 us  [per_device(): landed = lax.all_to_all(pieces, 'gyz', 1, 1, tiled=True)]
    all_to_all x0 -> x2, waiting for transfers between devices: none -> 12.7 us  [per_device(): landed = lax.all_to_all(pieces, 'gyz', 1, 1, tiled=True)]
    all_gather x1 -> x2, blocking collectives: 14.4 us -> 26.2 us  [per_device(): heads_along_x = lax.all_gather(flattened, 'gyx', axis=1, tiled=True)]
    all_to_all x1, blocking collectives: 27.3 us -> 36.9 us  [per_device(): own_block = lax.all_to_all(every_block, 'gyx', 0, 0, tiled=True)]
  transfers between devices with their start and end apart: 2 -> 6, of which waited for: 2 -> 5; matrix products, arithmetic and copies ran while one was open for 1% -> 16% of each run, Pallas kernels for 0% -> 0%
where the time goes in v5:
time: 318 us; the launch traced here: 314 us
  waiting for transfers between devices  138 us (43%)
  blocking collectives  90.9 us (29%)
  local copies, waits for them, and re-layouts  25.3 us (8%)
  matrix products  23.4 us (7%)
  starting transfers between devices  14.3 us (4%)
  between operations  13.7 us (4%)
  other arithmetic  9.04 us (3%)
    all_gather x2, waiting for transfers between devices, per_device(): gathered = lax.all_gather(piece, GY, axis=0, tiled=True)  88.2 us
    all_to_all x1, blocking collectives, per_device(): own_block = lax.all_to_all(every_block, 'gyx', 0, 0, tiled=True)  36.9 us
    reduce_scatter x2, waiting for transfers between devices, per_device(): lax.psum_scatter(jnp.concatenate([contract_rows(gathered, matrix) for mat...  35.9 us
    all_to_all x1, blocking collectives, gather_like_all_to_all(): return lax.all_to_all(copies, axis_name, 0, 0, tiled=True)  27.8 us
    all_gather x2, blocking collectives, per_device(): heads_along_x = lax.all_gather(flattened, 'gyx', axis=1, tiled=True)  26.2 us
    unnamed x42, local copies, waits for them, and re-layouts  16.7 us
    dot_general x10, matrix products, contract_rows(): lax.dot_general(left, right, (((1,), (1,)), ((), ())), preferred_element_...  14.6 us
    all_to_all x2, starting transfers between devices, per_device(): landed = lax.all_to_all(pieces, 'gyz', 1, 1, tiled=True)  14.2 us
  transfers between devices with their start and end apart: 6, of which 5 were waited for; matrix products, arithmetic and copies ran while one was open for 16% of the time, Pallas kernels for 0%

profile of v5, /device:TPU:8, one launch (start us, length us, event | category | flops | bytes accessed | tf_op | source)
XLA Modules:
  0.0 314.2 jit_solution(5586231267133242718)
XLA Ops:
  6.5 1.7 fusion.85
  9.1 82.6 %all-gather.5.cloned.1.call-done = bf16[1536,896]{1,0:T(8,128)(2,1)} async-done(((bf16[48,896]{1,0:T(8,128)(2,1)}), bf16[1536,896]{1,0:T(8,128)(2,1)}) %all-gather.5.cloned.1.call-update) | async-done | bytes 2752528 | tf_op jit(solution)/shard_map/all_gather | solution.py:118
  91.7 2.9 fusion.95
  96.8 1.0 fusion.94
  97.8 2.6 pad_maximum_fusion
  100.4 6.0 %copy.146 = f32[1536,800]{1,0:T(8,128)} copy(f32[1536,800]{0,1:T(8,128)} %pad_maximum_fusion) | data formatting | bytes 9830400
  107.4 27.8 %all_to_all.20 = bf16[8,224,448]{2,1,0:T(8,128)(2,1)S(1)} all-to-all(bf16[8,224,448]{2,1,0:T(8,128)(2,1)S(1)} %broadcast_in_dim.28), channel_id=1, replica_groups=mesh['gx'=8,'gyx'=4,'gyz'=8] {'gx'}, dimensions={0} | all-to-all | bytes 3211264 | tf_op jit(solution)/shard_map/all_to_all | solution.py:83
  135.2 36.9 %all_to_all.21 = bf16[4,2,224,448]{3,2,1,0:T(8,128)(2,1)S(1)} all-to-all(bf16[4,2,224,448]{3,2,1,0:T(8,128)(2,1)S(1)} %bitcast.228), channel_id=1, replica_groups=mesh['gx'=8,'gyx'=4,'gyz'=8] {'gyx'}, dimensions={0} | all-to-all | bytes 3211264 | tf_op jit(solution)/shard_map/all_to_all | solution.py:111
  172.1 5.6 %all-gather.7.cloned.1.call-done = bf16[1536,896]{1,0:T(8,128)(2,1)} async-done(((bf16[48,896]{1,0:T(8,128)(2,1)}), bf16[1536,896]{1,0:T(8,128)(2,1)}) %all-gather.7.cloned.1.call-update) | async-done | bytes 2752528 | tf_op jit(solution)/shard_map/all_gather | solution.py:118
  177.7 2.9 fusion.99
  183.8 2.6 pad_maximum_fusion.1
  186.4 6.1 %copy.148 = f32[1536,800]{1,0:T(8,128)} copy(f32[1536,800]{0,1:T(8,128)} %pad_maximum_fusion.1) | data formatting | bytes 9830400
  196.9 20.7 %reduce-scatter.7.cloned.1.call-done = f32[192,800]{1,0:T(8,128)} async-done(((f32[1536,800]{1,0:T(8,128)}), f32[192,800]{1,0:T(8,128)}) %reduce-scatter.7.cloned.1.call-update) | async-done | bytes 614416 | tf_op jit(solution)/shard_map/reduce_scatter | solution.py:121
  217.7 1.1 convert.12
  218.8 1.3 fusion.18
  224.1 13.2 %all-gather = bf16[4,224,192]{1,2,0:T(8,128)(2,1)S(1)} all-gather(bf16[1,224,192]{1,2,0:T(8,128)(2,1)S(1)} %bitcast.244), channel_id=1, replica_groups=mesh['gx'=8,'gyx'=4,'gyz'=8] {'gyx'}, dimensions={0}, use_global_device_ids=true | all-gather | bytes 430080 | tf_op jit(solution)/shard_map/all_gather | solution.py:147
  240.5 7.2 %all-to-all-start.2 = ((bf16[192,8,112]{2,0,1:T(8,128)(2,1)}), bf16[192,8,112]{2,0,1:T(8,128)(2,1)S(1)}, u32[]{:S(2)}, u32[]{:S(2)}) async-start(bf16[192,8,112]{2,0,1:T(8,128)(2,1)} %copy.113), calls=%async_computation.2 | async-start | bytes 786432 | tf_op jit(solution)/shard_map/all_to_all | solution.py:153
  247.7 15.1 %reduce-scatter.9.cloned.1.call-done = f32[192,800]{1,0:T(8,128)} async-done(((f32[1536,800]{1,0:T(8,128)}), f32[192,800]{1,0:T(8,128)}) %reduce-scatter.9.cloned.1.call-update) | async-done | bytes 614416 | tf_op jit(solution)/shard_map/reduce_scatter | solution.py:121
  262.8 1.1 convert.13
  264.1 1.3 fusion.19
  269.0 13.1 %all-gather.1 = bf16[4,224,192]{1,2,0:T(8,128)(2,1)S(1)} all-gather(bf16[1,224,192]{1,2,0:T(8,128)(2,1)S(1)} %bitcast.245), channel_id=1, replica_groups=mesh['gx'=8,'gyx'=4,'gyz'=8] {'gyx'}, dimensions={0}, use_global_device_ids=true | all-gather | bytes 430080 | tf_op jit(solution)/shard_map/all_gather | solution.py:147
  283.4 1.3 reshape.294
  287.0 7.0 %all-to-all-start.3 = ((bf16[192,8,112]{2,0,1:T(8,128)(2,1)}), bf16[192,8,112]{2,0,1:T(8,128)(2,1)S(1)}, u32[]{:S(2)}, u32[]{:S(2)}) async-start(bf16[192,8,112]{2,0,1:T(8,128)(2,1)} %copy.127), calls=%async_computation.3 | async-start | bytes 786432 | tf_op jit(solution)/shard_map/all_to_all | solution.py:153
  294.1 12.7 %all-to-all-done.3 = bf16[192,8,112]{2,0,1:T(8,128)(2,1)S(1)} async-done(((bf16[192,8,112]{2,0,1:T(8,128)(2,1)}), bf16[192,8,112]{2,0,1:T(8,128)(2,1)S(1)}, u32[]{:S(2)}, u32[]{:S(2)}) %all-to-all-start.3) | async-done | bytes 344096 | tf_op jit(solution)/shard_map/all_to_all | solution.py:153
  (114 shorter events, 26.7 us)
Async XLA Ops:
  6.5 213.6 %copy-start = (bf16[1,224,2048]{2,1,0:T(8,128)(2,1)S(1)}, bf16[1,224,2048]{2,1,0:T(8,128)(2,1)}, u32[]{:S(2)}) copy-start(bf16[1,224,2048]{2,1,0:T(8,128)(2,1)} %param.19) | copy-start | bytes 2752516
  6.5 85.1 %all-gather.5.cloned.1.call-start = ((), (), s32[]{:S(2)}) async-start(), calls=%async_computation.6 | async-start | bytes 2838528 | tf_op jit(solution)/shard_map/all_gather | solution.py:118
  8.2 169.5 %all-gather.7.cloned.1.call-start = ((), (), s32[]{:S(2)}) async-start(), calls=%async_computation.7 | async-start | bytes 2838528 | tf_op jit(solution)/shard_map/all_gather | solution.py:118
  9.0 85.6 %copy-start.3 = (bf16[224,896]{1,0:T(8,128)(2,1)S(1)}, bf16[224,896]{1,0:T(8,128)(2,1)}, u32[]{:S(2)}) copy-start(bf16[224,896]{1,0:T(8,128)(2,1)} %param.14) | copy-start | bytes 1204228
  9.0 208.7 %reduce-scatter.7.cloned.1.call-start = ((), (), s32[]{:S(2)}) async-start(), calls=%async_computation.8 | async-start | bytes 6193152 | tf_op jit(solution)/shard_map/reduce_scatter | solution.py:121
  91.7 3.0 copy-start.2
  94.6 1.1 copy-start.4
  95.7 1.1 copy-start.5
  106.3 0.9 copy-start.9
  106.4 156.4 %reduce-scatter.9.cloned.1.call-start = ((), (), s32[]{:S(2)}) async-start(), calls=%async_computation.9 | async-start | bytes 6193152 | tf_op jit(solution)/shard_map/reduce_scatter | solution.py:121
  177.7 2.9 copy-start.1
  181.7 1.1 copy-start.6
  192.5 0.7 copy-start.18
  193.9 24.9 %copy-start.7 = (bf16[224,128]{1,0:T(8,128)(2,1)S(1)}, bf16[224,128]{1,0:T(8,128)(2,1)}, u32[]{:S(2)}) copy-start(bf16[224,128]{1,0:T(8,128)(2,1)} %param.18) | copy-start | bytes 172036
  218.8 2.1 copy-start.12
  220.9 1.2 copy-start.16
  222.2 1.5 copy-start.14
  240.5 23.6 %copy-start.8 = (bf16[224,128]{1,0:T(8,128)(2,1)S(1)}, bf16[224,128]{1,0:T(8,128)(2,1)}, u32[]{:S(2)}) copy-start(bf16[224,128]{1,0:T(8,128)(2,1)} %param.18) | copy-start | bytes 172036
  240.5 46.5 %all-to-all-start.2 = ((bf16[192,8,112]{2,0,1:T(8,128)(2,1)}), bf16[192,8,112]{2,0,1:T(8,128)(2,1)S(1)}, u32[]{:S(2)}, u32[]{:S(2)}) async-start(bf16[192,8,112]{2,0,1:T(8,128)(2,1)} %copy.113), calls=%async_computation.2 | async-start | bytes 786432 | tf_op jit(solution)/shard_map/all_to_all | solution.py:153
  263.9 1.9 copy-start.13
  265.3 0.8 copy-start.10
  265.8 1.2 copy-start.17
  267.0 1.5 copy-start.15
  287.0 19.8 %all-to-all-start.3 = ((bf16[192,8,112]{2,0,1:T(8,128)(2,1)}), bf16[192,8,112]{2,0,1:T(8,128)(2,1)S(1)}, u32[]{:S(2)}, u32[]{:S(2)}) async-start(bf16[192,8,112]{2,0,1:T(8,128)(2,1)} %copy.127), calls=%async_computation.3 | async-start | bytes 786432 | tf_op jit(solution)/shard_map/all_to_all | solution.py:153
  (1 other events, 0.7 us)
Sparse Core Ops, SparseCore 0:
  9.9 81.6 all-gather.4
  94.3 83.4 all-gather.6
  180.3 37.3 reduce-scatter.6
  220.1 42.6 reduce-scatter.8

commit v6 on v5

--- a/solution.py
+++ b/solution.py
@@ -74,7 +74,7 @@
     return result.astype(jnp.bfloat16)
 
 
-CHUNKS = 2
+CHUNKS = 1
 
 
 def gather_like_all_to_all(block, axis_name):
@@ -109,7 +109,9 @@
     every_block = gather_like_all_to_all(out_weight, "gx")
     every_block = every_block.reshape(along_x, per_x, head_width, columns)
     own_block = lax.all_to_all(every_block, "gyx", 0, 0, tiled=True)
-    weights = (query_weight, key_weight, value_weight, adapter_down)
+    folded = jnp.dot(adapter_up, adapter_down, preferred_element_type=jnp.float32)
+    folded = (query_weight.astype(jnp.float32) + folded).astype(jnp.bfloat16)
+    weights = jnp.concatenate([folded, key_weight, value_weight], axis=0)
     local = inputs.shape[0]
     rows = local // CHUNKS
     results = []
@@ -117,18 +119,16 @@
         piece = inputs[chunk * rows : (chunk + 1) * rows]
         gathered = lax.all_gather(piece, GY, axis=0, tiled=True)
         if chunk == CHUNKS - 1:
-            gathered, own_block = lax.optimization_barrier((gathered, own_block))
+            gathered, own_block, weights = lax.optimization_barrier((gathered, own_block, weights))
         mixture = lax.psum_scatter(
-            jnp.concatenate([contract_rows(gathered, matrix) for matrix in weights], axis=1),
+            contract_rows(gathered, weights),
             "gx",
             scatter_dimension=0,
             tiled=True,
         )
-        query_base = mixture[:, :head_width]
+        queries = mixture[:, :head_width].astype(jnp.bfloat16)
         new_keys = mixture[:, head_width : 2 * head_width].astype(jnp.bfloat16)
-        new_values = mixture[:, 2 * head_width : 3 * head_width].astype(jnp.bfloat16)
-        adapter_mid = mixture[:, 3 * head_width :].astype(jnp.bfloat16)
-        queries = (query_base + contract_rows(adapter_mid, adapter_up)).astype(jnp.bfloat16)
+        new_values = mixture[:, 2 * head_width :].astype(jnp.bfloat16)
         requests = mixture.shape[0] // node_count
         shaped = (requests, node_count, head_count, HEAD)
         cached = (requests, head_count, HEAD, cache_keys.shape[2])

time: 318 us -> 218 us (0.69); the launches traced: 314 us -> 218 us
  waiting for transfers between devices: 138 us -> 103 us
  local copies, waits for them, and re-layouts: 25.3 us -> 2.42 us
  blocking collectives: 90.9 us -> 70 us
  starting transfers between devices: 14.3 us -> 4.58 us
  other arithmetic: 9.04 us -> 4.07 us
    all_gather x2 -> x1, waiting for transfers between devices: 88.2 us -> 34.1 us  [per_device(): gathered = lax.all_gather(piece, GY, axis=0, tiled=True)]
    unnamed x42 -> x18, local copies, waits for them, and re-layouts: 16.7 us -> 0.69 us
    all_gather x2 -> x1, blocking collectives: 26.2 us -> 14.4 us  [per_device(): heads_along_x = lax.all_gather(flattened, 'gyx', axis=1, tiled=True)]
    reduce_scatter x2 -> x1, waiting for transfers between devices: 35.9 us -> 45.9 us  [per_device(): lax.psum_scatter(contract_rows(gathered, weights), 'gx', scatter_dimensio...]
    all_to_all x1, blocking collectives: 36.9 us -> 27.2 us  [per_device(): landed = lax.all_to_all(pieces, 'gyz', 1, 1, tiled=True)]
    all_to_all x2 -> x1, starting transfers between devices: 14.2 us -> 4.54 us  [per_device(): own_block = lax.all_to_all(every_block, 'gyx', 0, 0, tiled=True)]
    all_to_all x2 -> x1, waiting for transfers between devices: 12.7 us -> 22 us  [per_device(): own_block = lax.all_to_all(every_block, 'gyx', 0, 0, tiled=True)]
    dot_general x10 -> x1, matrix products: 14.6 us -> 9.16 us  [contract_rows(): lax.dot_general(left, right, (((1,), (1,)), ((), ())), preferred_element_...]
  transfers between devices with their start and end apart: 6 -> 3, of which waited for: 5 -> 3; matrix products, arithmetic and copies ran while one was open for 16% -> 2% of each run, Pallas kernels for 0% -> 0%
where the time goes in v6:
time: 218 us
  waiting for transfers between devices  103 us (47%)
  blocking collectives  70 us (32%)
  matrix products  20.5 us (9%)
  between operations  13.7 us (6%)
  starting transfers between devices  4.58 us (2%)
  other arithmetic  4.07 us (2%)
  local copies, waits for them, and re-layouts  2.42 us (1%)
    reduce_scatter x1, waiting for transfers between devices, per_device(): lax.psum_scatter(contract_rows(gathered, weights), 'gx', scatter_dimensio...  45.9 us
    all_gather x1, waiting for transfers between devices, per_device(): gathered = lax.all_gather(piece, GY, axis=0, tiled=True)  34.1 us
    all_to_all x1, blocking collectives, gather_like_all_to_all(): return lax.all_to_all(copies, axis_name, 0, 0, tiled=True)  28.4 us
    all_to_all x1, blocking collectives, per_device(): landed = lax.all_to_all(pieces, 'gyz', 1, 1, tiled=True)  27.2 us
    all_to_all x1, waiting for transfers between devices, per_device(): own_block = lax.all_to_all(every_block, 'gyx', 0, 0, tiled=True)  22 us
    all_gather x1, blocking collectives, per_device(): heads_along_x = lax.all_gather(flattened, 'gyx', axis=1, tiled=True)  14.4 us
    dot_general x1, matrix products, contract_rows(): lax.dot_general(left, right, (((1,), (1,)), ((), ())), preferred_element_...  9.16 us
    all_to_all x1, starting transfers between devices, per_device(): own_block = lax.all_to_all(every_block, 'gyx', 0, 0, tiled=True)  4.54 us
  transfers between devices with their start and end apart: 3, of which 3 were waited for; matrix products, arithmetic and copies ran while one was open for 2% of the time, Pallas kernels for 0%

profile of v6, /device:TPU:8, one launch (start us, length us, event | category | flops | bytes accessed | tf_op | source)
XLA Modules:
  0.0 218.0 jit_solution(15827629615756202001)
XLA Ops:
  6.5 0.7 all-gather.2.cloned.1.call-update
  7.3 1.1 broadcast_in_dim.17
  8.4 28.4 %all_to_all.15 = bf16[8,224,448]{2,1,0:T(8,128)(2,1)} all-to-all(bf16[8,224,448]{2,1,0:T(8,128)(2,1)S(1)} %broadcast_in_dim.17), channel_id=1, replica_groups=mesh['gx'=8,'gyx'=4,'gyz'=8] {'gx'}, dimensions={0} | all-to-all | bytes 3211264 | tf_op jit(solution)/shard_map/all_to_all | solution.py:83
  36.8 4.5 %all-to-all-start.1 = ((bf16[4,2,224,448]{3,2,1,0:T(8,128)(2,1)}), bf16[4,2,224,448]{3,2,1,0:T(8,128)(2,1)}, u32[]{:S(2)}, u32[]{:S(2)}) async-start(bf16[4,2,224,448]{3,2,1,0:T(8,128)(2,1)} %bitcast.120), calls=%async_computation.1 | async-start | bytes 3670016 | tf_op jit(solution)/shard_map/all_to_all | solution.py:111
  41.7 1.1 pad_maximum_fusion
  42.8 22.0 %all-to-all-done.1 = bf16[4,2,224,448]{3,2,1,0:T(8,128)(2,1)} async-done(((bf16[4,2,224,448]{3,2,1,0:T(8,128)(2,1)}), bf16[4,2,224,448]{3,2,1,0:T(8,128)(2,1)}, u32[]{:S(2)}, u32[]{:S(2)}) %all-to-all-start.1) | async-done | bytes 1605664 | tf_op jit(solution)/shard_map/all_to_all | solution.py:111
  64.8 34.1 %all-gather.2.cloned.1.call-done = bf16[3072,896]{1,0:T(8,128)(2,1)} async-done(((bf16[96,896]{1,0:T(8,128)(2,1)}), bf16[3072,896]{1,0:T(8,128)(2,1)}) %all-gather.2.cloned.1.call-update) | async-done | bytes 5505040 | tf_op jit(solution)/shard_map/all_gather | solution.py:120
  98.9 9.2 %fusion.44 = f32[3072,672]{0,1:T(8,128)} fusion(bf16[3072,896]{1,0:T(8,128)(2,1)} %all-gather.2.cloned.1.call-done, bf16[672,896]{1,0:T(8,128)(2,1)S(1)} %pad_maximum_fusion), kind=kOutput, calls=%fused_computation.68 | convolution fusion | flops 3699376128 | bytes 14966784 | tf_op jit(solution)/shard_map/dot_general | solution.py:15
  108.1 0.6 copy-done.8
  108.7 0.4 fusion.15
  109.1 0.3 fusion.16
  109.7 0.3 fusion.18
  110.4 0.3 fusion.24
  110.8 45.9 %reduce-scatter.2.cloned.1.call-done = f32[384,672]{0,1:T(8,128)} async-done(((f32[3072,672]{0,1:T(8,128)}), f32[384,672]{0,1:T(8,128)}) %reduce-scatter.2.cloned.1.call-update) | async-done | bytes 1032208 | tf_op jit(solution)/shard_map/reduce_scatter | solution.py:123
  156.7 1.3 convert.6
  158.4 1.8 bitcast_reduce_fusion
  160.4 0.5 fusion.43
  161.3 0.6 fusion.1
  162.1 3.0 %fusion.9 = f32[8,48,1,224]{3,1,0,2:T(8,128)S(1)} fusion(f32[8,48]{1,0:T(8,128)S(1)} %add_add_fusion, f32[8,48]{1,0:T(8,128)S(1)} %maximum_maximum_fusion, f32[8,48,2048]{2,1,0:T(8,128)} %copy-done.1, bf16[1,224,2048]{2,1,0:T(8,128)(2,1)} %param.20), kind=kOutput, calls=%fused_computation.17 | convolution fusion | flops 354680832 | bytes 4410368 | tf_op jit(solution)/shard_map/rnhp,hep->rnhe/dot_general | solution.py:67
  165.3 0.7 fusion.14
  166.2 14.4 %all_gather.7 = bf16[384,896]{0,1:T(8,128)(2,1)S(1)} all-gather(bf16[384,224]{0,1:T(8,128)(2,1)S(1)} %copy.49), channel_id=1, replica_groups=mesh['gx'=8,'gyx'=4,'gyz'=8] {'gyx'}, dimensions={1}, use_global_device_ids=true | all-gather | bytes 860160 | tf_op jit(solution)/shard_map/all_gather | solution.py:147
  180.6 2.6 %fusion.4 = bf16[384,2,448]{0,2,1:T(8,128)(2,1)S(1)} fusion(bf16[384,4,224,1]{0,2,3,1:T(8,128)(2,1)S(1)} %bitcast.126, bf16[4,2,224,448]{3,2,1,0:T(8,128)(2,1)} %all-to-all-done.1), kind=kOutput, calls=%fused_computation.9 | convolution fusion | flops 616906752 | bytes 2981888 | tf_op jit(solution)/shard_map/txe,xkec->tkc/dot_general | solution.py:149
  183.2 27.2 %all_to_all.16 = bf16[384,8,112]{0,2,1:T(8,128)(2,1)S(1)} all-to-all(bf16[384,8,112]{0,2,1:T(8,128)(2,1)S(1)} %bitcast.125), channel_id=1, replica_groups=mesh['gx'=8,'gyx'=4,'gyz'=8] {'gyz'}, dimensions={1} | all-to-all | bytes 1376256 | tf_op jit(solution)/shard_map/all_to_all | solution.py:153
  210.4 0.7 reduce_sum.42
  (36 shorter events, 2.5 us)
Async XLA Ops:
  6.5 153.9 %copy-start = (bf16[8,224,512]{2,1,0:T(8,128)(2,1)S(1)}, bf16[8,224,512]{2,1,0:T(8,128)(2,1)}, u32[]{:S(2)}) copy-start(bf16[8,224,512]{2,1,0:T(8,128)(2,1)} %param.21) | copy-start | bytes 5505028
  6.5 92.3 %all-gather.2.cloned.1.call-start = ((), (), s32[]{:S(2)}) async-start(), calls=%async_computation.4 | async-start | bytes 5677056 | tf_op jit(solution)/shard_map/all_gather | solution.py:120
  36.8 4.6 %copy-start.3 = (bf16[224,896]{1,0:T(8,128)(2,1)S(1)}, bf16[224,896]{1,0:T(8,128)(2,1)}, u32[]{:S(2)}) copy-start(bf16[224,896]{1,0:T(8,128)(2,1)} %param.14) | copy-start | bytes 1204228
  36.8 4.6 %copy-start.4 = (bf16[128,896]{1,0:T(8,128)(2,1)S(1)}, bf16[128,896]{1,0:T(8,128)(2,1)}, u32[]{:S(2)}) copy-start(bf16[128,896]{1,0:T(8,128)(2,1)} %param.17) | copy-start | bytes 688132
  36.8 4.6 %copy-start.5 = (bf16[224,128]{1,0:T(8,128)(2,1)S(1)}, bf16[224,128]{1,0:T(8,128)(2,1)}, u32[]{:S(2)}) copy-start(bf16[224,128]{1,0:T(8,128)(2,1)} %param.18) | copy-start | bytes 172036
  36.8 4.9 %copy-start.2 = (bf16[224,896]{1,0:T(8,128)(2,1)S(1)}, bf16[224,896]{1,0:T(8,128)(2,1)}, u32[]{:S(2)}) copy-start(bf16[224,896]{1,0:T(8,128)(2,1)} %param.16) | copy-start | bytes 1204228
  36.8 28.0 %all-to-all-start.1 = ((bf16[4,2,224,448]{3,2,1,0:T(8,128)(2,1)}), bf16[4,2,224,448]{3,2,1,0:T(8,128)(2,1)}, u32[]{:S(2)}, u32[]{:S(2)}) async-start(bf16[4,2,224,448]{3,2,1,0:T(8,128)(2,1)} %bitcast.120), calls=%async_computation.1 | async-start | bytes 3670016 | tf_op jit(solution)/shard_map/all_to_all | solution.py:111
  41.3 115.4 %reduce-scatter.2.cloned.1.call-start = ((), (), s32[]{:S(2)}) async-start(), calls=%async_computation.5 | async-start | bytes 9289728 | tf_op jit(solution)/shard_map/reduce_scatter | solution.py:123
  108.0 0.7 copy-start.8
  108.1 2.6 %copy-start.6 = (s32[8]{0:T(128)S(1)}, s32[8]{0:T(128)}, u32[]{:S(2)}) copy-start(s32[8]{0:T(128)} %param.23) | copy-start | bytes 100
  160.2 1.7 copy-start.1
  162.0 3.2 %copy-start.7 = (bf16[8,224,512]{2,1,0:T(8,128)(2,1)S(1)}, bf16[8,224,512]{2,1,0:T(8,128)(2,1)}, u32[]{:S(2)}) copy-start(bf16[8,224,512]{2,1,0:T(8,128)(2,1)} %param.22) | copy-start | bytes 5505028
Sparse Core Ops, SparseCore 0:
  9.9 88.9 all-gather.1
  108.2 48.4 reduce-scatter.1

commit v7 on v6

--- a/solution.py
+++ b/solution.py
@@ -144,10 +144,9 @@
             parents[chunk::CHUNKS],
         )
         flattened = attended.reshape(requests * node_count, head_width)
-        heads_along_x = lax.all_gather(flattened, "gyx", axis=1, tiled=True)
-        heads_along_x = heads_along_x.reshape(requests * node_count, along_x, head_width)
+        heads_along_x = gather_like_all_to_all(flattened, "gyx")
         partial_sums = jnp.einsum(
-            "txe,xkec->tkc", heads_along_x, own_block, preferred_element_type=jnp.float32
+            "xte,xkec->tkc", heads_along_x, own_block, preferred_element_type=jnp.float32
         )
         pieces = partial_sums.astype(jnp.bfloat16).reshape(requests * node_count, along_z, -1)
         landed = lax.all_to_all(pieces, "gyz", 1, 1, tiled=True)

time: 218 us -> 220 us (level)
  matrix products: 20.5 us -> 17.2 us
  blocking collectives: 70 us -> 73.3 us
    all_to_all x1 -> x2, blocking collectives: 28.4 us -> 45.3 us  [gather_like_all_to_all(): return lax.all_to_all(copies, axis_name, 0, 0, tiled=True)]
    all_gather x1 -> x0, blocking collectives: 14.4 us -> none  [per_device(): heads_along_x = lax.all_gather(flattened, 'gyx', axis=1, tiled=True)]
    dot_general x1, matrix products: 2.95 us -> 0.74 us  [attend(): jnp.einsum('rnhp,hep->rnhe', w_prompt, prompt_v, preferred_element_type=j...]
where the time goes in v7:
time: 220 us
  waiting for transfers between devices  103 us (47%)
  blocking collectives  73.3 us (33%)
  matrix products  17.2 us (8%)
  between operations  13.7 us (6%)
  starting transfers between devices  4.58 us (2%)
  other arithmetic  4.08 us (2%)
  local copies, waits for them, and re-layouts  3.99 us (2%)
    reduce_scatter x1, waiting for transfers between devices, per_device(): lax.psum_scatter(contract_rows(gathered, weights), 'gx', scatter_dimensio...  45.9 us
    all_to_all x2, blocking collectives, gather_like_all_to_all(): return lax.all_to_all(copies, axis_name, 0, 0, tiled=True)  45.3 us
    all_gather x1, waiting for transfers between devices, per_device(): gathered = lax.all_gather(piece, GY, axis=0, tiled=True)  34.1 us
    all_to_all x1, blocking collectives, per_device(): landed = lax.all_to_all(pieces, 'gyz', 1, 1, tiled=True)  28 us
    all_to_all x1, waiting for transfers between devices, per_device(): own_block = lax.all_to_all(every_block, 'gyx', 0, 0, tiled=True)  22 us
    dot_general x1, matrix products, contract_rows(): lax.dot_general(left, right, (((1,), (1,)), ((), ())), preferred_element_...  9.28 us
    all_to_all x1, starting transfers between devices, per_device(): own_block = lax.all_to_all(every_block, 'gyx', 0, 0, tiled=True)  4.54 us
  transfers between devices with their start and end apart: 3, of which 3 were waited for; matrix products, arithmetic and copies ran while one was open for 2% of the time, Pallas kernels for 0%

profile of v7, /device:TPU:8, one launch (start us, length us, event | category | flops | bytes accessed | tf_op | source)
XLA Modules:
  0.0 219.6 jit_solution(2637664804992328352)
XLA Ops:
  6.5 0.7 all-gather.2.cloned.1.call-update
  7.3 1.1 broadcast_in_dim.22
  8.4 28.4 %all_to_all.20 = bf16[8,224,448]{2,1,0:T(8,128)(2,1)} all-to-all(bf16[8,224,448]{2,1,0:T(8,128)(2,1)S(1)} %broadcast_in_dim.22), channel_id=1, replica_groups=mesh['gx'=8,'gyx'=4,'gyz'=8] {'gx'}, dimensions={0} | all-to-all | bytes 3211264 | tf_op jit(solution)/shard_map/all_to_all | solution.py:83
  36.8 4.5 %all-to-all-start.1 = ((bf16[4,2,224,448]{3,2,1,0:T(8,128)(2,1)}), bf16[4,2,224,448]{3,2,1,0:T(8,128)(2,1)}, u32[]{:S(2)}, u32[]{:S(2)}) async-start(bf16[4,2,224,448]{3,2,1,0:T(8,128)(2,1)} %bitcast.119), calls=%async_computation.1 | async-start | bytes 3670016 | tf_op jit(solution)/shard_map/all_to_all | solution.py:111
  41.7 1.1 pad_maximum_fusion
  42.8 22.0 %all-to-all-done.1 = bf16[4,2,224,448]{3,2,1,0:T(8,128)(2,1)} async-done(((bf16[4,2,224,448]{3,2,1,0:T(8,128)(2,1)}), bf16[4,2,224,448]{3,2,1,0:T(8,128)(2,1)}, u32[]{:S(2)}, u32[]{:S(2)}) %all-to-all-start.1) | async-done | bytes 1605664 | tf_op jit(solution)/shard_map/all_to_all | solution.py:111
  64.8 34.1 %all-gather.2.cloned.1.call-done = bf16[3072,896]{1,0:T(8,128)(2,1)} async-done(((bf16[96,896]{1,0:T(8,128)(2,1)}), bf16[3072,896]{1,0:T(8,128)(2,1)}) %all-gather.2.cloned.1.call-update) | async-done | bytes 5505040 | tf_op jit(solution)/shard_map/all_gather | solution.py:120
  98.9 9.3 %fusion.45 = f32[3072,672]{0,1:T(8,128)} fusion(bf16[3072,896]{1,0:T(8,128)(2,1)} %all-gather.2.cloned.1.call-done, bf16[672,896]{1,0:T(8,128)(2,1)S(1)} %pad_maximum_fusion), kind=kOutput, calls=%fused_computation.69 | convolution fusion | flops 3699376128 | bytes 14966784 | tf_op jit(solution)/shard_map/dot_general | solution.py:15
  108.2 0.6 copy-done.10
  108.8 0.4 fusion.15
  110.5 0.3 fusion.24
  110.9 45.9 %reduce-scatter.2.cloned.1.call-done = f32[384,672]{0,1:T(8,128)} async-done(((f32[3072,672]{0,1:T(8,128)}), f32[384,672]{0,1:T(8,128)}) %reduce-scatter.2.cloned.1.call-update) | async-done | bytes 1032208 | tf_op jit(solution)/shard_map/reduce_scatter | solution.py:123
  156.8 1.3 convert.6
  158.2 0.8 copy.35
  159.3 0.7 bitcast_reduce_fusion
  160.2 0.5 fusion.44
  160.8 0.6 fusion.1
  162.0 0.7 fusion.9
  162.8 0.8 copy-done.8
  163.5 0.7 fusion.14
  164.5 16.9 %all_to_all.21 = bf16[4,384,224]{1,2,0:T(8,128)(2,1)S(1)} all-to-all(bf16[4,384,224]{1,2,0:T(8,128)(2,1)S(1)} %broadcast_in_dim.27), channel_id=1, replica_groups=mesh['gx'=8,'gyx'=4,'gyz'=8] {'gyx'}, dimensions={0} | all-to-all | bytes 1376256 | tf_op jit(solution)/shard_map/all_to_all | solution.py:83
  181.4 2.6 %fusion.4 = bf16[384,2,448]{0,2,1:T(8,128)(2,1)S(1)} fusion(bf16[4,2,224,448]{3,2,1,0:T(8,128)(2,1)} %all-to-all-done.1, bf16[4,384,224]{1,2,0:T(8,128)(2,1)S(1)} %all_to_all.21), kind=kOutput, calls=%fused_computation.9 | convolution fusion | flops 616906752 | bytes 2981888 | tf_op jit(solution)/shard_map/xte,xkec->tkc/dot_general | solution.py:148
  184.0 28.0 %all_to_all.22 = bf16[384,8,112]{0,2,1:T(8,128)(2,1)S(1)} all-to-all(bf16[384,8,112]{0,2,1:T(8,128)(2,1)S(1)} %bitcast.124), channel_id=1, replica_groups=mesh['gx'=8,'gyx'=4,'gyz'=8] {'gyz'}, dimensions={1} | all-to-all | bytes 1376256 | tf_op jit(solution)/shard_map/all_to_all | solution.py:152
  212.0 0.7 reduce_sum.42
  (41 shorter events, 3.1 us)
Async XLA Ops:
  6.5 153.7 %copy-start = (bf16[8,224,512]{2,1,0:T(8,128)(2,1)S(1)}, bf16[8,224,512]{2,1,0:T(8,128)(2,1)}, u32[]{:S(2)}) copy-start(bf16[8,224,512]{2,1,0:T(8,128)(2,1)} %param.21) | copy-start | bytes 5505028
  6.5 92.3 %all-gather.2.cloned.1.call-start = ((), (), s32[]{:S(2)}) async-start(), calls=%async_computation.5 | async-start | bytes 5677056 | tf_op jit(solution)/shard_map/all_gather | solution.py:120
  36.8 4.6 %copy-start.3 = (bf16[224,896]{1,0:T(8,128)(2,1)S(1)}, bf16[224,896]{1,0:T(8,128)(2,1)}, u32[]{:S(2)}) copy-start(bf16[224,896]{1,0:T(8,128)(2,1)} %param.14) | copy-start | bytes 1204228
  36.8 4.6 %copy-start.4 = (bf16[128,896]{1,0:T(8,128)(2,1)S(1)}, bf16[128,896]{1,0:T(8,128)(2,1)}, u32[]{:S(2)}) copy-start(bf16[128,896]{1,0:T(8,128)(2,1)} %param.17) | copy-start | bytes 688132
  36.8 4.6 %copy-start.6 = (bf16[224,128]{1,0:T(8,128)(2,1)S(1)}, bf16[224,128]{1,0:T(8,128)(2,1)}, u32[]{:S(2)}) copy-start(bf16[224,128]{1,0:T(8,128)(2,1)} %param.18) | copy-start | bytes 172036
  36.8 4.9 %copy-start.2 = (bf16[224,896]{1,0:T(8,128)(2,1)S(1)}, bf16[224,896]{1,0:T(8,128)(2,1)}, u32[]{:S(2)}) copy-start(bf16[224,896]{1,0:T(8,128)(2,1)} %param.16) | copy-start | bytes 1204228
  36.8 28.0 %all-to-all-start.1 = ((bf16[4,2,224,448]{3,2,1,0:T(8,128)(2,1)}), bf16[4,2,224,448]{3,2,1,0:T(8,128)(2,1)}, u32[]{:S(2)}, u32[]{:S(2)}) async-start(bf16[4,2,224,448]{3,2,1,0:T(8,128)(2,1)} %bitcast.119), calls=%async_computation.1 | async-start | bytes 3670016 | tf_op jit(solution)/shard_map/all_to_all | solution.py:111
  41.3 115.5 %reduce-scatter.2.cloned.1.call-start = ((), (), s32[]{:S(2)}) async-start(), calls=%async_computation.6 | async-start | bytes 9289728 | tf_op jit(solution)/shard_map/reduce_scatter | solution.py:123
  108.2 0.7 copy-start.10
  108.2 2.6 %copy-start.7 = (s32[8]{0:T(128)S(1)}, s32[8]{0:T(128)}, u32[]{:S(2)}) copy-start(s32[8]{0:T(128)} %param.23) | copy-start | bytes 100
  110.2 49.1 %copy-start.1 = (bf16[1,224,2048]{2,1,0:T(8,128)(2,1)S(1)}, bf16[1,224,2048]{2,1,0:T(8,128)(2,1)}, u32[]{:S(2)}) copy-start(bf16[1,224,2048]{2,1,0:T(8,128)(2,1)} %param.19) | copy-start | bytes 2752516
  160.7 0.9 copy-start.5
  160.8 1.2 copy-start.9
  162.0 1.5 copy-start.8
Sparse Core Ops, SparseCore 0:
  9.9 88.9 all-gather.1
  108.3 48.4 reduce-scatter.1

commit v8 on v7

--- a/solution.py
+++ b/solution.py
@@ -107,8 +107,10 @@
     per_x = groups // along_x
     columns = out_weight.shape[1]
     every_block = gather_like_all_to_all(out_weight, "gx")
-    every_block = every_block.reshape(along_x, per_x, head_width, columns)
-    own_block = lax.all_to_all(every_block, "gyx", 0, 0, tiled=True)
+    width = columns * groups // (along_x * along_z)
+    every_block = every_block.reshape(along_x, per_x, head_width, columns // width, width)
+    sent = every_block.transpose(1, 3, 0, 2, 4).reshape(along_z, along_x, head_width, width)
+    own_block = lax.all_to_all(sent, "gyz", 0, 0, tiled=True)
     folded = jnp.dot(adapter_up, adapter_down, preferred_element_type=jnp.float32)
     folded = (query_weight.astype(jnp.float32) + folded).astype(jnp.bfloat16)
     weights = jnp.concatenate([folded, key_weight, value_weight], axis=0)
@@ -144,12 +146,12 @@
             parents[chunk::CHUNKS],
         )
         flattened = attended.reshape(requests * node_count, head_width)
-        heads_along_x = gather_like_all_to_all(flattened, "gyx")
+        heads_along_z = lax.all_gather(flattened, "gyz", axis=0)
         partial_sums = jnp.einsum(
-            "xte,xkec->tkc", heads_along_x, own_block, preferred_element_type=jnp.float32
+            "zte,zxec->txc", heads_along_z, own_block, preferred_element_type=jnp.float32
         )
-        pieces = partial_sums.astype(jnp.bfloat16).reshape(requests * node_count, along_z, -1)
-        landed = lax.all_to_all(pieces, "gyz", 1, 1, tiled=True)
+        pieces = partial_sums.astype(jnp.bfloat16)
+        landed = lax.all_to_all(pieces, "gyx", 1, 1, tiled=True)
         out = jnp.sum(landed.astype(jnp.float32), axis=1).astype(jnp.bfloat16)
         results.append(out.reshape(requests, node_count, -1))
     stacked = jnp.stack(results, axis=1)

time: 220 us -> 247 us (1.12)
  waiting for transfers between devices: 103 us -> 158 us
  blocking collectives: 73.3 us -> 39 us
  starting transfers between devices: 4.58 us -> 8.69 us
    all_gather x0 -> x1, waiting for transfers between devices: none -> 41.4 us  [per_device(): heads_along_z = lax.all_gather(flattened, 'gyz', axis=0)]
    all_to_all x1, waiting for transfers between devices: 22 us -> 57.3 us  [per_device(): own_block = lax.all_to_all(sent, 'gyz', 0, 0, tiled=True)]
    all_gather x1, waiting for transfers between devices: 34.1 us -> 12.1 us  [per_device(): gathered = lax.all_gather(piece, GY, axis=0, tiled=True)]
    all_to_all x2 -> x1, blocking collectives: 45.3 us -> 27.8 us  [gather_like_all_to_all(): return lax.all_to_all(copies, axis_name, 0, 0, tiled=True)]
    all_to_all x1, blocking collectives: 28 us -> 11.2 us  [per_device(): landed = lax.all_to_all(pieces, 'gyx', 1, 1, tiled=True)]
    all_to_all x1, starting transfers between devices: 4.54 us -> 8.61 us  [per_device(): own_block = lax.all_to_all(sent, 'gyz', 0, 0, tiled=True)]
  transfers between devices with their start and end apart: 3 -> 4, of which waited for: 3 -> 4; matrix products, arithmetic and copies ran while one was open for 2% -> 2% of each run, Pallas kernels for 0% -> 0%
where the time goes in v8:
time: 247 us
  waiting for transfers between devices  158 us (64%)
  blocking collectives  39 us (16%)
  matrix products  17.5 us (7%)
  between operations  13.4 us (5%)
  starting transfers between devices  8.69 us (4%)
  local copies, waits for them, and re-layouts  6.11 us (2%)
  other arithmetic  4.04 us (2%)
    all_to_all x1, waiting for transfers between devices, per_device(): own_block = lax.all_to_all(sent, 'gyz', 0, 0, tiled=True)  57.3 us
    reduce_scatter x1, waiting for transfers between devices, per_device(): lax.psum_scatter(contract_rows(gathered, weights), 'gx', scatter_dimensio...  46.5 us
    all_gather x1, waiting for transfers between devices, per_device(): heads_along_z = lax.all_gather(flattened, 'gyz', axis=0)  41.4 us
    all_to_all x1, blocking collectives, gather_like_all_to_all(): return lax.all_to_all(copies, axis_name, 0, 0, tiled=True)  27.8 us
    all_gather x1, waiting for transfers between devices, per_device(): gathered = lax.all_gather(piece, GY, axis=0, tiled=True)  12.1 us
    all_to_all x1, blocking collectives, per_device(): landed = lax.all_to_all(pieces, 'gyx', 1, 1, tiled=True)  11.2 us
    dot_general x1, matrix products, contract_rows(): lax.dot_general(left, right, (((1,), (1,)), ((), ())), preferred_element_...  9.27 us
    all_to_all x1, starting transfers between devices, per_device(): own_block = lax.all_to_all(sent, 'gyz', 0, 0, tiled=True)  8.61 us
  transfers between devices with their start and end apart: 4, of which 4 were waited for; matrix products, arithmetic and copies ran while one was open for 2% of the time, Pallas kernels for 0%

profile of v8, /device:TPU:8, one launch (start us, length us, event | category | flops | bytes accessed | tf_op | source)
XLA Modules:
  0.0 246.9 jit_solution(12704699217811051856)
XLA Ops:
  6.5 0.7 all-gather.3.cloned.1.call-update
  7.3 1.1 copy.52
  8.5 27.8 %all_to_all.15 = bf16[8,224,448]{1,2,0:T(8,128)(2,1)S(1)} all-to-all(bf16[8,224,448]{1,2,0:T(8,128)(2,1)S(1)} %broadcast_in_dim.17), channel_id=1, replica_groups=mesh['gx'=8,'gyx'=4,'gyz'=8] {'gx'}, dimensions={0} | all-to-all | bytes 3211264 | tf_op jit(solution)/shard_map/all_to_all | solution.py:83
  36.3 1.4 copy.53
  37.7 8.6 %all-to-all-start.1 = ((bf16[8,4,224,112]{2,3,1,0:T(8,128)(2,1)}), bf16[8,4,224,112]{2,3,1,0:T(8,128)(2,1)}, u32[]{:S(2)}, u32[]{:S(2)}) async-start(bf16[8,4,224,112]{2,3,1,0:T(8,128)(2,1)} %copy.53), calls=%async_computation.1 | async-start | bytes 3670016 | tf_op jit(solution)/shard_map/all_to_all | solution.py:113
  46.7 1.1 pad_maximum_fusion
  47.8 57.3 %all-to-all-done.1 = bf16[8,4,224,112]{2,3,1,0:T(8,128)(2,1)} async-done(((bf16[8,4,224,112]{2,3,1,0:T(8,128)(2,1)}), bf16[8,4,224,112]{2,3,1,0:T(8,128)(2,1)}, u32[]{:S(2)}, u32[]{:S(2)}) %all-to-all-start.1) | async-done | bytes 1605664 | tf_op jit(solution)/shard_map/all_to_all | solution.py:113
  105.1 12.1 %all-gather.3.cloned.1.call-done = bf16[3072,896]{1,0:T(8,128)(2,1)} async-done(((bf16[96,896]{1,0:T(8,128)(2,1)}), bf16[3072,896]{1,0:T(8,128)(2,1)}) %all-gather.3.cloned.1.call-update) | async-done | bytes 5505040 | tf_op jit(solution)/shard_map/all_gather | solution.py:122
  117.2 9.3 %fusion.51 = f32[3072,672]{0,1:T(8,128)} fusion(bf16[3072,896]{1,0:T(8,128)(2,1)} %all-gather.3.cloned.1.call-done, bf16[672,896]{1,0:T(8,128)(2,1)S(1)} %pad_maximum_fusion), kind=kOutput, calls=%fused_computation.70 | convolution fusion | flops 3699376128 | bytes 14966784 | tf_op jit(solution)/shard_map/dot_general | solution.py:15
  126.6 0.6 copy-done.10
  129.3 46.5 %reduce-scatter.2.cloned.1.call-done = f32[384,672]{0,1:T(8,128)} async-done(((f32[3072,672]{0,1:T(8,128)}), f32[384,672]{0,1:T(8,128)}) %reduce-scatter.2.cloned.1.call-update) | async-done | bytes 1032208 | tf_op jit(solution)/shard_map/reduce_scatter | solution.py:125
  175.8 1.3 convert.6
  177.1 0.8 copy.62
  178.3 0.7 bitcast_reduce_fusion
  179.1 0.5 fusion.50
  179.8 0.6 fusion.1
  181.0 0.7 fusion.16
  181.8 0.8 copy-done.8
  182.5 0.7 fusion.21
  183.3 0.8 copy.64
  184.1 41.4 %all-gather.5.cloned.1.call-done = bf16[8,384,224]{1,2,0:T(8,128)(2,1)} async-done(((bf16[1,384,224]{1,2,0:T(8,128)(2,1)}), bf16[8,384,224]{1,2,0:T(8,128)(2,1)}) %all-gather.5.cloned.1.call-update) | async-done | bytes 1376272 | tf_op jit(solution)/shard_map/all_gather | solution.py:149
  225.5 3.0 %fusion.13 = bf16[384,4,112]{0,2,1:T(8,128)(2,1)S(1)} fusion(bf16[8,4,224,112]{2,3,1,0:T(8,128)(2,1)} %all-to-all-done.1, bf16[8,384,224]{1,2,0:T(8,128)(2,1)} %all-gather.5.cloned.1.call-done), kind=kOutput, calls=%fused_computation.17 | convolution fusion | flops 616734720 | bytes 3325952 | tf_op jit(solution)/shard_map/zte,zxec->txc/dot_general | solution.py:150
  228.5 11.2 %all_to_all.16 = bf16[384,4,112]{0,2,1:T(8,128)(2,1)S(1)} all-to-all(bf16[384,4,112]{0,2,1:T(8,128)(2,1)S(1)} %fusion.13), channel_id=1, replica_groups=mesh['gx'=8,'gyx'=4,'gyz'=8] {'gyx'}, dimensions={1} | all-to-all | bytes 688128 | tf_op jit(solution)/shard_map/all_to_all | solution.py:154
  239.7 0.7 reduce_sum.42
  (44 shorter events, 3.9 us)
Async XLA Ops:
  6.5 172.6 %copy-start = (bf16[8,224,512]{2,1,0:T(8,128)(2,1)S(1)}, bf16[8,224,512]{2,1,0:T(8,128)(2,1)}, u32[]{:S(2)}) copy-start(bf16[8,224,512]{2,1,0:T(8,128)(2,1)} %param.21) | copy-start | bytes 5505028
  6.5 110.7 %all-gather.3.cloned.1.call-start = ((), (), s32[]{:S(2)}) async-start(), calls=%async_computation.4 | async-start | bytes 5677056 | tf_op jit(solution)/shard_map/all_gather | solution.py:122
  37.7 8.7 %copy-start.3 = (bf16[224,896]{1,0:T(8,128)(2,1)S(1)}, bf16[224,896]{1,0:T(8,128)(2,1)}, u32[]{:S(2)}) copy-start(bf16[224,896]{1,0:T(8,128)(2,1)} %param.14) | copy-start | bytes 1204228
  37.7 8.7 %copy-start.4 = (bf16[128,896]{1,0:T(8,128)(2,1)S(1)}, bf16[128,896]{1,0:T(8,128)(2,1)}, u32[]{:S(2)}) copy-start(bf16[128,896]{1,0:T(8,128)(2,1)} %param.17) | copy-start | bytes 688132
  37.7 8.7 %copy-start.6 = (bf16[224,128]{1,0:T(8,128)(2,1)S(1)}, bf16[224,128]{1,0:T(8,128)(2,1)}, u32[]{:S(2)}) copy-start(bf16[224,128]{1,0:T(8,128)(2,1)} %param.18) | copy-start | bytes 172036
  37.7 9.0 %copy-start.2 = (bf16[224,896]{1,0:T(8,128)(2,1)S(1)}, bf16[224,896]{1,0:T(8,128)(2,1)}, u32[]{:S(2)}) copy-start(bf16[224,896]{1,0:T(8,128)(2,1)} %param.16) | copy-start | bytes 1204228
  37.7 67.4 %all-to-all-start.1 = ((bf16[8,4,224,112]{2,3,1,0:T(8,128)(2,1)}), bf16[8,4,224,112]{2,3,1,0:T(8,128)(2,1)}, u32[]{:S(2)}, u32[]{:S(2)}) async-start(bf16[8,4,224,112]{2,3,1,0:T(8,128)(2,1)} %copy.53), calls=%async_computation.1 | async-start | bytes 3670016 | tf_op jit(solution)/shard_map/all_to_all | solution.py:113
  46.4 129.4 %reduce-scatter.2.cloned.1.call-start = ((), (), s32[]{:S(2)}) async-start(), calls=%async_computation.5 | async-start | bytes 9289728 | tf_op jit(solution)/shard_map/reduce_scatter | solution.py:125
  126.5 0.7 copy-start.10
  126.5 2.6 %copy-start.7 = (s32[8]{0:T(128)S(1)}, s32[8]{0:T(128)}, u32[]{:S(2)}) copy-start(s32[8]{0:T(128)} %param.23) | copy-start | bytes 100
  126.6 99.0 %all-gather.5.cloned.1.call-start = ((), (), s32[]{:S(2)}) async-start(), calls=%async_computation.6 | async-start | bytes 1548288 | tf_op jit(solution)/shard_map/all_gather | solution.py:149
  129.3 49.0 %copy-start.1 = (bf16[1,224,2048]{2,1,0:T(8,128)(2,1)S(1)}, bf16[1,224,2048]{2,1,0:T(8,128)(2,1)}, u32[]{:S(2)}) copy-start(bf16[1,224,2048]{2,1,0:T(8,128)(2,1)} %param.19) | copy-start | bytes 2752516
  179.7 0.9 copy-start.5
  179.8 1.3 copy-start.9
  181.0 1.5 copy-start.8
Sparse Core Ops, SparseCore 0:
  9.9 107.2 all-gather.2
  126.7 49.0 reduce-scatter.1
  184.2 41.2 all-gather.4
